TPU v7x, 32 devices: a whole 2x2x4 slice. The times are simulated.
32 devices in a mesh: req: 8 (over y, x, core), tp: 4 (over z).
Axes of the slice: x: 2, y: 2, z: 4, core: 2. Of those that a mesh axis runs over, the one named last changes fastest.
Arguments:
- final_states: float32 [16384, 1024], P('req'), may hold values from -50 to 50
- norm_gain: float32 [1024], replicated, may hold values from 0.1 to 1.9
- embedding: bfloat16 [32768, 1024], P('tp'), may hold values from -2 to 2
- targets: int32 [16384], P('req'), may hold values from 0 to 32767
- deal: int32 [8192], P('req'), may hold values from 0 to 16383, as said below
Outputs:
- logprob: float32 [16384], P('req')
- entropy: float32 [16384], P('req')
Inputs may be any that keep to these rules, and one draw needn't show every extreme that they name: Every owned row is named at most once. The rows named of each owner device are a prefix of its 2048 rows (its sequence's live tokens), between 128 and 2048 rows long, and some owner device is named in full; the rest is padding. Each owner's live rows are dealt over all req devices, its own device included. Along each device's 8192 // 8 positions, in order, the owner device number deal // 2048 never decreases. At most 256 positions of one device name rows of one owner device, and some device reaches 256.
All inputs are finite; a program needn't handle non-finite values.
Results may differ from a plain program's by a relative error of at most 0.0031.
Values sent between devices are 32-bit elements; how exact they have to be, the bound alone decides.
No kernel may reach another device: no remote copies, remote signals or barrier semaphores. Data moves between devices by JAX's collectives and lax.ppermute only.
A program may use at most 128 MiB of HBM per device.

v0:
```python
import jax
import jax.numpy as jnp
from jax import lax
from jax.sharding import PartitionSpec as P


def rms_normed(states, norm_gain):
    mean_square = jnp.mean(states * states, axis=1, keepdims=True)
    return (states * lax.rsqrt(mean_square + 1e-06) * norm_gain[None, :]).astype(jnp.bfloat16)


def body(final_states, norm_gain, embedding, targets, deal):
    owners = lax.axis_size("req")
    own_rows = final_states.shape[0]
    capacity = own_rows // owners
    positions = deal.shape[0]
    shard_cols = embedding.shape[0]
    vocab_start = lax.axis_index("tp") * shard_cols
    source = deal // own_rows
    local_row = deal % own_rows
    member = (source[:, None] == jnp.arange(owners, dtype=jnp.int32)[None, :]).astype(jnp.int32)
    counts = jnp.sum(member, axis=0)
    starts = jnp.cumsum(counts) - counts
    offset = jnp.arange(positions, dtype=jnp.int32) - jnp.sum(member * starts[None, :], axis=1)
    slot_index = source * capacity + offset
    asked_rows = jnp.full((owners * capacity,), -1, jnp.int32).at[slot_index].set(local_row)
    wanted = lax.all_to_all(asked_rows, "req", split_axis=0, concat_axis=0, tiled=True)
    is_live = wanted >= 0
    picked = jnp.where(is_live, wanted, 0)
    outgoing_rows = jnp.where(is_live[:, None], final_states[picked], 0.0)
    arrived = lax.all_to_all(outgoing_rows, "req", split_axis=0, concat_axis=0, tiled=True)
    scored_rows = arrived[slot_index]
    owned_normed = rms_normed(final_states, norm_gain)
    in_shard_id = targets - vocab_start
    inside = (in_shard_id >= 0) & (in_shard_id < shard_cols)
    target_rows = embedding[jnp.clip(in_shard_id, 0, shard_cols - 1)]
    target_term = jnp.einsum(
        "rd,rd->r", owned_normed, target_rows, preferred_element_type=jnp.float32
    )
    owner_chosen = lax.psum(jnp.where(inside, target_term, 0.0), "tp")
    normed = rms_normed(scored_rows, norm_gain)
    logits = lax.dot_general(
        normed, embedding, (((1,), (1,)), ((), ())), preferred_element_type=jnp.float32
    )
    local_peak = jnp.max(logits, axis=1)
    row_peak = lax.pmax(local_peak, "tp")
    weights = jnp.exp(logits - row_peak[:, None])
    local_sums = jnp.stack((jnp.sum(weights, axis=1), jnp.sum(weights * logits, axis=1)))
    sums_all = lax.psum(local_sums, "tp")
    log_total = row_peak + jnp.log(sums_all[0])
    expected = sums_all[1] / sums_all[0]
    result_rows = jnp.stack((log_total, expected))
    outgoing = jnp.zeros((2, owners * capacity), jnp.float32).at[:, slot_index].set(result_rows)
    returned = lax.all_to_all(outgoing, "req", split_axis=1, concat_axis=1, tiled=True)
    home_row = jnp.where(is_live, wanted, own_rows)

    def to_owner(values):
        return jnp.zeros((own_rows,), jnp.float32).at[home_row].set(values, mode="drop")

    live_rows = to_owner(jnp.ones((owners * capacity,), jnp.float32))
    log_owned = to_owner(returned[0])
    expected_owned = to_owner(returned[1])
    logprob = (owner_chosen - log_owned) * live_rows
    entropy = log_owned - expected_owned
    return (logprob, entropy)


def solution(mesh):
    return jax.shard_map(
        body,
        mesh=mesh,
        in_specs=(P("req", None), P(), P("tp", None), P("req"), P("req")),
        out_specs=(P("req"), P("req")),
        check_vma=False,
    )
```

profile of v0, /device:TPU:0, one launch (start us, length us, event | category | flops | bytes accessed | tf_op | source)
XLA Modules:
  0.0 251.2 jit_solution(6436493523009157254)
XLA Ops:
  0.6 0.7 add_select_fusion.1
  1.7 0.7 broadcast_clamp_fusion.1
  2.4 4.3 %scatter_custom_fusion = s32[2048]{0:T(1024)S(1)} fusion(s32[1024]{0:T(1024)S(1)} %get-tuple-element.7, s32[1024]{0:T(1024)S(1)} %get-tuple-element.16, s32[]{:T(128)} %constant.57.clone.1), kind=kCustom, calls=%fused_computation.49 | custom fusion | bytes 8196 | tf_op jit(solution)/shard_map/scatter | solution.py:26
  6.8 9.7 %all_to_all.30 = s32[8,256,1]{1,2,0:T(1,128)S(1)} all-to-all(s32[8,256,1]{1,2,0:T(1,128)S(1)} %bitcast.25), channel_id=1, replica_groups=mesh['req'=8,'tp'=4] {'req'}, dimensions={0} | all-to-all | bytes 16384 | tf_op jit(solution)/shard_map/all_to_all | solution.py:27
  16.5 15.1 %gather_fusion.1 = f32[2048,1024]{1,0:T(8,128)} fusion(f32[2048,1024]{1,0:T(8,128)} %param.5, s32[2048]{0:T(1024)S(1)} %broadcast_clamp_fusion), kind=kCustom, calls=%fused_computation.1 | custom fusion | bytes 16785408 | tf_op jit(solution)/shard_map/gather | solution.py:30
  31.6 5.8 %broadcast_select_fusion = f32[8,256,1024]{2,1,0:T(8,128)} fusion(f32[8,256,1024]{2,1,0:T(8,128)} %bitcast.21, pred[8,256]{1,0:T(8,128)(4,1)S(1)} %fusion.8), kind=kLoop, calls=%fused_computation.17 | loop fusion | flops 2097152 | bytes 16779264 | tf_op jit(solution)/shard_map/jit(_where)/select_n | solution.py:30
  37.4 5.3 %all-to-all-start.1 = ((f32[8,256,1024]{2,1,0:T(8,128)}), f32[8,256,1024]{2,1,0:T(8,128)}, u32[]{:S(2)}, u32[]{:S(2)}) async-start(f32[8,256,1024]{2,1,0:T(8,128)} %broadcast_select_fusion), calls=%async_computation.1 | async-start | bytes 16777216 | tf_op jit(solution)/shard_map/all_to_all | solution.py:31
  42.7 18.9 %gather_fusion = bf16[2048,1024]{1,0:T(8,128)(2,1)} fusion(bf16[8192,1024]{1,0:T(8,128)(2,1)} %param.7, s32[2048]{0:T(1024)S(1)} %fusion.7), kind=kCustom, calls=%fused_computation | custom fusion | bytes 8396800 | tf_op jit(solution)/shard_map/gather | solution.py:36
  61.7 4.1 %multiply_reduce_fusion.1 = f32[2048]{0:T(1024)S(1)} fusion(f32[2048,1024]{1,0:T(8,128)} %param.5), kind=kLoop, calls=%fused_computation.14 | loop fusion | flops 4192256 | bytes 8396800 | tf_op jit(solution)/shard_map/reduce_sum | solution.py:8
  66.2 4.4 %fusion.1 = f32[2048]{0:T(1024)S(1)} fusion(bf16[2048,1024]{1,0:T(8,128)(2,1)S(1)} %copy-done, f32[2048,1024]{1,0:T(8,128)} %param.5, f32[1024]{0:T(1024)S(1)} %copy-done.2, f32[2048]{0:T(1024)S(1)} %add_rsqrt_fusion), kind=kLoop, calls=%fused_computation.12 | loop fusion | flops 14678016 | bytes 12603392 | tf_op jit(solution)/shard_map/rd,rd->r/dot_general | solution.py:37
  70.6 66.0 %all-to-all-done.1 = f32[8,256,1024]{2,1,0:T(8,128)} async-done(((f32[8,256,1024]{2,1,0:T(8,128)}), f32[8,256,1024]{2,1,0:T(8,128)}, u32[]{:S(2)}, u32[]{:S(2)}) %all-to-all-start.1) | async-done | bytes 8388640 | tf_op jit(solution)/shard_map/all_to_all | solution.py:31
  136.6 9.8 %gather_fusion.2 = f32[1024,1024]{1,0:T(8,128)} fusion(f32[2048,1024]{1,0:T(8,128)} %bitcast.8, s32[1024]{0:T(1024)S(1)} %get-tuple-element.6), kind=kCustom, calls=%fused_computation.2 | custom fusion | bytes 8392704 | tf_op jit(solution)/shard_map/gather | solution.py:32
  146.3 2.5 %multiply_reduce_fusion.2 = f32[1024]{0:T(1024)S(1)} fusion(f32[1024,1024]{1,0:T(8,128)} %gather_fusion.2), kind=kLoop, calls=%fused_computation.16 | loop fusion | flops 2096128 | bytes 4198400 | tf_op jit(solution)/shard_map/reduce_sum | solution.py:8
  148.9 26.7 %fusion.21 = (f32[1024]{0:T(1024)S(1)}, f32[1024,8192]{1,0:T(8,128)}) fusion(bf16[8192,1024]{1,0:T(8,128)(2,1)} %param.7, f32[1024,1024]{1,0:T(8,128)} %gather_fusion.2, f32[1024]{0:T(1024)S(1)} %copy-done.2, f32[1024]{0:T(1024)S(1)} %add_rsqrt_fusion.1), kind=kOutput, calls=%fused_computation.64 | convolution fusion | flops 17191403520 | bytes 54538240 | tf_op jit(solution)/shard_map/dot_general | solution.py:42
  175.6 11.9 %pmax.7 = f32[1024]{0:T(1024)S(1)} all-reduce(f32[1024]{0:T(1024)S(1)} %get-tuple-element.17), channel_id=1, replica_groups=mesh['req'=8,'tp'=4] {'tp'}, use_global_device_ids=true, to_apply=%region_8.9 | all-reduce | flops 1024 | bytes 8192 | tf_op jit(solution)/shard_map/pmax | solution.py:46
  187.5 15.2 %fusion = (f32[1024]{0:T(1024)S(1)}, f32[1024]{0:T(1024)S(1)}) fusion(f32[1024,8192]{1,0:T(8,128)} %get-tuple-element.18, f32[1024]{0:T(1024)S(1)} %pmax.7), kind=kLoop, calls=%fused_computation.10 | loop fusion | flops 33552384 | bytes 33566720 | tf_op jit(solution)/shard_map/reduce_sum | solution.py:48
  202.7 15.8 %all-reduce = (f32[2048]{0:T(1024)S(1)}, f32[2,1024]{1,0:T(2,128)S(1)}) all-reduce(f32[2048]{0:T(1024)S(1)} %and_select_fusion, f32[2,1024]{1,0:T(2,128)S(1)} %pad_maximum_fusion), channel_id=1, replica_groups=mesh['req'=8,'tp'=4] {'tp'}, use_global_device_ids=true, to_apply=%region_1.2 | all-reduce | flops 4096 | bytes 32768 | tf_op jit(solution)/shard_map/psum | solution.py:40
  218.8 3.3 %scatter_custom_fusion.1 = f32[2,2048]{0,1:T(8,128)S(1)} fusion(s32[1024]{0:T(1024)S(1)} %get-tuple-element.7, f32[1024,2]{1,0:T(8,128)S(1)} %copy.15, f32[]{:T(128)} %constant.27.clone.1), kind=kCustom, calls=%fused_computation.21 | custom fusion | bytes 16388 | tf_op jit(solution)/shard_map/scatter | solution.py:53
  222.2 0.9 copy.16
  223.1 3.3 %all-to-all-start.2 = ((f32[2,8,256]{2,0,1:T(2,128)}), f32[2,8,256]{2,0,1:T(2,128)S(1)}, u32[]{:S(2)}, u32[]{:S(2)}) async-start(f32[2,8,256]{2,0,1:T(2,128)} %copy.16), calls=%async_computation.2 | async-start | bytes 32768 | tf_op jit(solution)/shard_map/all_to_all | solution.py:54
  226.4 8.0 %scatter_custom_fusion.3 = f32[2048]{0:T(1024)S(1)} fusion(s32[2048]{0:T(1024)S(1)} %bitcast.30, f32[2048]{0:T(1024)S(1)} %broadcast.120, f32[]{:T(128)} %constant.27.clone.1), kind=kCustom, calls=%fused_computation.53 | custom fusion | bytes 8196 | tf_op jit(solution)/shard_map/scatter | solution.py:58
  234.5 8.0 %scatter_custom_fusion.4 = f32[2048]{0:T(1024)S(1)} fusion(s32[2048]{0:T(1024)S(1)} %bitcast.31, f32[2048]{0:T(1024)S(1)} %bitcast.34, f32[]{:T(128)} %constant.27.clone.1), kind=kCustom, calls=%fused_computation.51 | custom fusion | bytes 8196 | tf_op jit(solution)/shard_map/scatter | solution.py:58
  242.6 8.0 %scatter_custom_fusion.2 = f32[2048]{0:T(1024)S(1)} fusion(s32[2048]{0:T(1024)S(1)} %bitcast.32, f32[2048]{0:T(1024)S(1)} %bitcast.33, f32[]{:T(128)} %constant.27.clone.1), kind=kCustom, calls=%fused_computation.55 | custom fusion | bytes 8196 | tf_op jit(solution)/shard_map/scatter | solution.py:58
  250.6 0.6 fusion.20
  (25 shorter events, 1.2 us)
Async XLA Ops:
  37.4 5.3 %copy-start.1 = (s32[2048]{0:T(1024)S(1)}, s32[2048]{0:T(1024)}, u32[]{:S(2)}) copy-start(s32[2048]{0:T(1024)} %param.8) | copy-start | bytes 24580
  37.4 99.2 %all-to-all-start.1 = ((f32[8,256,1024]{2,1,0:T(8,128)}), f32[8,256,1024]{2,1,0:T(8,128)}, u32[]{:S(2)}, u32[]{:S(2)}) async-start(f32[8,256,1024]{2,1,0:T(8,128)} %broadcast_select_fusion), calls=%async_computation.1 | async-start | bytes 16777216 | tf_op jit(solution)/shard_map/all_to_all | solution.py:31
  61.7 4.6 %copy-start = (bf16[2048,1024]{1,0:T(8,128)(2,1)S(1)}, bf16[2048,1024]{1,0:T(8,128)(2,1)}, u32[]{:S(2)}) copy-start(bf16[2048,1024]{1,0:T(8,128)(2,1)} %gather_fusion) | copy-start | bytes 12582916
  61.7 4.6 %copy-start.2 = (f32[1024]{0:T(1024)S(1)}, f32[1024]{0:T(1024)}, u32[]{:S(2)}) copy-start(f32[1024]{0:T(1024)} %param.6) | copy-start | bytes 12292
  223.1 11.4 %all-to-all-start.2 = ((f32[2,8,256]{2,0,1:T(2,128)}), f32[2,8,256]{2,0,1:T(2,128)S(1)}, u32[]{:S(2)}, u32[]{:S(2)}) async-start(f32[2,8,256]{2,0,1:T(2,128)} %copy.16), calls=%async_computation.2 | async-start | bytes 32768 | tf_op jit(solution)/shard_map/all_to_all | solution.py:54
where the time goes:
time: 252 us; the launch traced here: 251 us
  local copies, waits for them, and re-layouts  77.2 us (31%)
  waiting for transfers between devices  66 us (26%)
  blocking collectives  37.4 us (15%)
  other arithmetic  34.6 us (14%)
  matrix products  26.7 us (11%)
  starting transfers between devices  8.61 us (3%)
    all_to_all x1, waiting for transfers between devices, body(): lax.all_to_all(outgoing_rows, 'req', split_axis=0, concat_axis=0, tiled=T...  66 us
    dot_general x1, matrix products, body(): lax.dot_general(normed, embedding, (((1,), (1,)), ((), ())), preferred_el...  26.7 us
    scatter x3, local copies, waits for them, and re-layouts, to_owner(): jnp.zeros((own_rows,), jnp.float32).at[home_row].set(values, mode='drop')  24.1 us
    gather x1, local copies, waits for them, and re-layouts, body(): target_rows = embedding[jnp.clip(in_shard_id, 0, shard_cols - 1)]  18.9 us
    psum x1, blocking collectives, body(): owner_chosen = lax.psum(jnp.where(inside, target_term, 0.0), 'tp')  15.8 us
    reduce_sum x1, other arithmetic, body(): jnp.sum(weights, axis=1)  15.2 us
    gather x1, local copies, waits for them, and re-layouts, body(): outgoing_rows = jnp.where(is_live[:, None], final_states[picked], 0.0)  15.1 us
    pmax x1, blocking collectives, body(): row_peak = lax.pmax(local_peak, 'tp')  11.9 us
  transfers between devices with their start and end apart: 2, of which 1 were waited for; matrix products, arithmetic and copies ran while one was open for 14% of the time, Pallas kernels for 0%

commit v1 on v0

v1 whole, which is shorter than its diff:
```python
import jax
import jax.numpy as jnp
from jax import lax
from jax.sharding import PartitionSpec as P


def rms_normed(states, norm_gain):
    mean_square = jnp.mean(states * states, axis=1, keepdims=True)
    return (states * lax.rsqrt(mean_square + 1e-06) * norm_gain[None, :]).astype(jnp.bfloat16)


def shard_stats(normed, embedding, in_shard_id):
    logits = lax.dot_general(
        normed, embedding, (((1,), (1,)), ((), ())), preferred_element_type=jnp.float32
    )
    peak = jnp.max(logits, axis=1)
    weights = jnp.exp(logits - peak[:, None])
    total = jnp.sum(weights, axis=1)
    moment = jnp.sum(weights * logits, axis=1)
    cols = lax.broadcasted_iota(jnp.int32, logits.shape, 1)
    chosen = jnp.sum(jnp.where(cols == in_shard_id[:, None], logits, 0.0), axis=1)
    return jnp.stack((peak, total, moment, chosen))


def body(final_states, norm_gain, embedding, targets, deal):
    owners = lax.axis_size("req")
    own_rows = final_states.shape[0]
    shard_cols = embedding.shape[0]
    vocab_start = lax.axis_index("tp") * shard_cols
    member = (deal[:, None] // own_rows == jnp.arange(owners, dtype=jnp.int32)[None, :])
    counts = lax.psum(jnp.sum(member.astype(jnp.int32), axis=0), "req")
    live_count = counts[lax.axis_index("req")]
    live = jnp.arange(own_rows, dtype=jnp.int32) < live_count

    in_shard_id = targets - vocab_start
    block = 512 if own_rows % 512 == 0 else own_rows
    parts = []
    for b in range(own_rows // block):
        rows = slice(b * block, (b + 1) * block)
        normed = rms_normed(final_states[rows], norm_gain)
        parts.append(shard_stats(normed, embedding, in_shard_id[rows]))
    stats = jnp.concatenate(parts, axis=1)
    gathered = lax.all_gather(stats, "tp")
    peaks = gathered[:, 0]
    row_peak = jnp.max(peaks, axis=0)
    scale = jnp.exp(peaks - row_peak[None, :])
    exp_total = jnp.sum(gathered[:, 1] * scale, axis=0)
    moment = jnp.sum(gathered[:, 2] * scale, axis=0)
    chosen = jnp.sum(gathered[:, 3], axis=0)
    log_total = row_peak + jnp.log(exp_total)
    expected = moment / exp_total
    logprob = jnp.where(live, chosen - log_total, 0.0)
    entropy = jnp.where(live, log_total - expected, 0.0)
    return (logprob, entropy)


def solution(mesh):
    return jax.shard_map(
        body,
        mesh=mesh,
        in_specs=(P("req", None), P(), P("tp", None), P("req"), P("req")),
        out_specs=(P("req"), P("req")),
        check_vma=False,
    )
```

time: 252 us -> 134 us (0.53)
  local copies, waits for them, and re-layouts: 77.2 us -> 0.59 us
  waiting for transfers between devices: 66 us -> 0 us
  matrix products: 26.7 us -> 65.8 us
  blocking collectives: 37.4 us -> 23.1 us
  other arithmetic: 34.6 us -> 43.9 us
  starting transfers between devices: 8.61 us -> 0 us
    all_to_all x2 -> x0, waiting for transfers between devices: 66 us -> none  [the longest x1 66 us: body(): lax.all_to_all(outgoing_rows, 'req', split_axis=0, concat_axis=0, tiled=T...]
    gather x3 -> x0, local copies, waits for them, and re-layouts: 43.8 us -> none  [the longest x1 18.9 us: body(): target_rows = embedding[jnp.clip(in_shard_id, 0, shard_cols - 1)]]
    dot_general x1 -> x4, matrix products: 26.7 us -> 65.8 us  [shard_stats(): lax.dot_general(normed, embedding, (((1,), (1,)), ((), ())), preferred_el...]
    scatter x5 -> x0, local copies, waits for them, and re-layouts: 31.8 us -> none  [the longest x3 24.1 us: to_owner(): jnp.zeros((own_rows,), jnp.float32).at[home_row].set(values, mode='drop')]
    reduce_sum x3 -> x6, other arithmetic: 15.4 us -> 37.1 us  [the longest x4 36.9 us: shard_stats(): total = jnp.sum(weights, axis=1)]
    all_gather x0 -> x1, blocking collectives: none -> 13.6 us  [body(): gathered = lax.all_gather(stats, 'tp')]
    pmax x1 -> x0, blocking collectives: 11.9 us -> none  [body(): row_peak = lax.pmax(local_peak, 'tp')]
    all_to_all x1 -> x0, blocking collectives: 9.67 us -> none  [body(): lax.all_to_all(asked_rows, 'req', split_axis=0, concat_axis=0, tiled=True)]
  transfers between devices with their start and end apart: 2 -> 0, of which waited for: 1 -> 0; matrix products, arithmetic and copies ran while one was open for 14% -> 0% of each run, Pallas kernels for 0% -> 0%
where the time goes in v1:
time: 134 us
  matrix products  65.8 us (49%)
  other arithmetic  43.9 us (33%)
  blocking collectives  23.1 us (17%)
    dot_general x4, matrix products, shard_stats(): lax.dot_general(normed, embedding, (((1,), (1,)), ((), ())), preferred_el...  65.8 us
    reduce_sum x4, other arithmetic, shard_stats(): total = jnp.sum(weights, axis=1)  36.9 us
    all_gather x1, blocking collectives, body(): gathered = lax.all_gather(stats, 'tp')  13.6 us
    psum x1, blocking collectives, body(): counts = lax.psum(jnp.sum(member.astype(jnp.int32), axis=0), 'req')  9.47 us
    reduce_sum x1, other arithmetic, rms_normed(): mean_square = jnp.mean(states * states, axis=1, keepdims=True)  4.09 us

profile of v1, /device:TPU:0, one launch (start us, length us, event | category | flops | bytes accessed | tf_op | source)
XLA Modules:
  0.0 134.0 jit_solution(11715956837336508926)
XLA Ops:
  0.6 0.7 add_select_fusion
  1.3 0.1 convert_reduce_fusion
  1.5 9.5 %psum.7 = s32[8]{0:T(128)S(1)} all-reduce(s32[8]{0:T(128)S(1)} %convert_reduce_fusion), channel_id=1, replica_groups=mesh['req'=8,'tp'=4] {'req'}, use_global_device_ids=true, to_apply=%region_1.2 | all-reduce | flops 8 | bytes 64 | tf_op jit(solution)/shard_map/psum | solution.py:31
  10.9 0.6 dynamic_slice.3
  11.5 0.7 broadcast_subtract_fusion
  12.2 4.1 %multiply_reduce_fusion.7 = (f32[512]{0:T(512)S(1)}, f32[512]{0:T(512)S(1)}, f32[512]{0:T(512)S(1)}, f32[512]{0:T(512)S(1)}) fusion(f32[2048,1024]{1,0:T(8,128)} %param.5), kind=kLoop, calls=%fused_computation.27 | loop fusion | flops 4192256 | bytes 8396800 | tf_op jit(solution)/shard_map/reduce_sum | solution.py:8
  16.3 16.4 %fusion.25 = (f32[512]{0:T(512)S(1)}, f32[512,8192]{1,0:T(8,128)}) fusion(bf16[8192,1024]{1,0:T(8,128)(2,1)} %param.7, f32[2048,1024]{1,0:T(8,128)} %param.5, f32[512]{0:T(512)S(1)} %get-tuple-element.41, f32[1024]{0:T(1024)} %param.6), kind=kOutput, calls=%fused_computation.71 | convolution fusion | flops 8595701760 | bytes 35659776 | tf_op jit(solution)/shard_map/dot_general | solution.py:13
  32.7 0.0 copy-start
  32.7 9.2 %fusion = (f32[512]{0:T(512)S(1)}, f32[512]{0:T(512)S(1)}, f32[512]{0:T(512)S(1)}) fusion(f32[512,8192]{1,0:T(8,128)} %get-tuple-element.34, f32[512]{0:T(512)S(1)} %get-tuple-element.33, s32[512]{0:T(512)S(1)} %get-tuple-element.30), kind=kLoop, calls=%fused_computation.4 | loop fusion | flops 29358592 | bytes 16787456 | tf_op jit(solution)/shard_map/reduce_sum | solution.py:18
  42.0 0.0 copy-done
  42.0 16.4 %fusion.27 = (f32[512]{0:T(512)S(1)}, f32[512,8192]{1,0:T(8,128)}) fusion(bf16[8192,1024]{1,0:T(8,128)(2,1)} %param.7, f32[2048,1024]{1,0:T(8,128)} %param.5, f32[512]{0:T(512)S(1)} %get-tuple-element.43, f32[1024]{0:T(1024)S(1)} %copy-done), kind=kOutput, calls=%fused_computation.73 | convolution fusion | flops 8595701760 | bytes 35659776 | tf_op jit(solution)/shard_map/dot_general | solution.py:13
  58.4 9.2 %fusion.2 = (f32[512]{0:T(512)S(1)}, f32[512]{0:T(512)S(1)}, f32[512]{0:T(512)S(1)}) fusion(f32[512,8192]{1,0:T(8,128)} %get-tuple-element.38, f32[512]{0:T(512)S(1)} %get-tuple-element.37, s32[512]{0:T(512)S(1)} %get-tuple-element.32), kind=kLoop, calls=%fused_computation.14 | loop fusion | flops 29358592 | bytes 16787456 | tf_op jit(solution)/shard_map/reduce_sum | solution.py:18
  67.6 16.6 %fusion.26 = (f32[512]{0:T(512)S(1)}, f32[512,8192]{1,0:T(8,128)}) fusion(bf16[8192,1024]{1,0:T(8,128)(2,1)} %param.7, f32[2048,1024]{1,0:T(8,128)} %param.5, f32[512]{0:T(512)S(1)} %get-tuple-element.42, f32[1024]{0:T(1024)S(1)} %copy-done), kind=kOutput, calls=%fused_computation.72 | convolution fusion | flops 8595701760 | bytes 35659776 | tf_op jit(solution)/shard_map/dot_general | solution.py:13
  84.2 9.2 %fusion.1 = (f32[512]{0:T(512)S(1)}, f32[512]{0:T(512)S(1)}, f32[512]{0:T(512)S(1)}) fusion(f32[512,8192]{1,0:T(8,128)} %get-tuple-element.36, f32[512]{0:T(512)S(1)} %get-tuple-element.35, s32[512]{0:T(512)S(1)} %get-tuple-element.31), kind=kLoop, calls=%fused_computation.9 | loop fusion | flops 29358592 | bytes 16787456 | tf_op jit(solution)/shard_map/reduce_sum | solution.py:18
  93.4 16.4 %fusion.28 = (f32[512]{0:T(512)S(1)}, f32[512,8192]{1,0:T(8,128)}) fusion(bf16[8192,1024]{1,0:T(8,128)(2,1)} %param.7, f32[2048,1024]{1,0:T(8,128)} %param.5, f32[1024]{0:T(1024)S(1)} %copy-done, f32[512]{0:T(512)S(1)} %get-tuple-element.44), kind=kOutput, calls=%fused_computation.74 | convolution fusion | flops 8595701760 | bytes 35659776 | tf_op jit(solution)/shard_map/dot_general | solution.py:13
  109.8 9.2 %fusion.3 = (f32[512]{0:T(512)S(1)}, f32[512]{0:T(512)S(1)}, f32[512]{0:T(512)S(1)}) fusion(f32[512,8192]{1,0:T(8,128)} %get-tuple-element.40, f32[512]{0:T(512)S(1)} %get-tuple-element.39, s32[512]{0:T(512)S(1)} %get-tuple-element.29), kind=kLoop, calls=%fused_computation.19 | loop fusion | flops 29358592 | bytes 16787456 | tf_op jit(solution)/shard_map/reduce_sum | solution.py:18
  119.0 13.6 %all-gather.1 = f32[4,4,2048]{2,1,0:T(4,128)S(1)} all-gather(f32[1,4,2048]{2,1,0:T(4,128)S(1)} %maximum_bitcast_fusion), channel_id=2, replica_groups=mesh['req'=8,'tp'=4] {'tp'}, dimensions={0}, use_global_device_ids=true | all-gather | bytes 163840 | tf_op jit(solution)/shard_map/all_gather | solution.py:43
  132.6 0.1 fusion.23
  132.8 0.1 fusion.17
  132.8 1.2 subtract_select_fusion
  (4 shorter events, 0.1 us)
Async XLA Ops:
  32.7 9.2 %copy-start = (f32[1024]{0:T(1024)S(1)}, f32[1024]{0:T(1024)}, u32[]{:S(2)}) copy-start(f32[1024]{0:T(1024)} %param.6) | copy-start | bytes 12292

commit v2 on v1

--- a/solution.py
+++ b/solution.py
@@ -1,6 +1,10 @@
+import functools
+
 import jax
 import jax.numpy as jnp
 from jax import lax
+from jax.experimental import pallas as pl
+from jax.experimental.pallas import tpu as pltpu
 from jax.sharding import PartitionSpec as P
 
 
@@ -9,7 +13,7 @@
     return (states * lax.rsqrt(mean_square + 1e-06) * norm_gain[None, :]).astype(jnp.bfloat16)
 
 
-def shard_stats(normed, embedding, in_shard_id):
+def shard_stats_xla(normed, embedding, in_shard_id):
     logits = lax.dot_general(
         normed, embedding, (((1,), (1,)), ((), ())), preferred_element_type=jnp.float32
     )
@@ -22,24 +26,85 @@
     return jnp.stack((peak, total, moment, chosen))
 
 
+def stats_kernel(row_block, normed_ref, emb_ref, ids_ref, peak_ref, total_ref, moment_ref, chosen_ref):
+    j = pl.program_id(0)
+    col_block = emb_ref.shape[0]
+
+    @pl.when(j == 0)
+    def _():
+        peak_ref[...] = jnp.full(peak_ref.shape, -1e30, jnp.float32)
+        total_ref[...] = jnp.zeros(total_ref.shape, jnp.float32)
+        moment_ref[...] = jnp.zeros(moment_ref.shape, jnp.float32)
+        chosen_ref[...] = jnp.zeros(chosen_ref.shape, jnp.float32)
+
+    table = emb_ref[...]
+    cols = lax.broadcasted_iota(jnp.int32, (row_block, col_block), 1)
+
+    def chunk(r, carry):
+        rows = pl.ds(pl.multiple_of(r * row_block, row_block), row_block)
+        logits = lax.dot_general(
+            normed_ref[rows, :], table, (((1,), (1,)), ((), ())),
+            preferred_element_type=jnp.float32,
+        )
+        old_peak = peak_ref[rows, :]
+        new_peak = jnp.maximum(old_peak, jnp.max(logits, axis=1, keepdims=True))
+        weights = jnp.exp(logits - new_peak)
+        scale = jnp.exp(old_peak - new_peak)
+        total_ref[rows, :] = total_ref[rows, :] * scale + jnp.sum(weights, axis=1, keepdims=True)
+        moment_ref[rows, :] = moment_ref[rows, :] * scale + jnp.sum(
+            weights * logits, axis=1, keepdims=True
+        )
+        peak_ref[rows, :] = new_peak
+        local_id = ids_ref[rows, :] - j * col_block
+        chosen_ref[rows, :] = chosen_ref[rows, :] + jnp.sum(
+            jnp.where(cols == local_id, logits, 0.0), axis=1, keepdims=True
+        )
+        return carry
+
+    lax.fori_loop(0, normed_ref.shape[0] // row_block, chunk, 0)
+
+
+def shard_stats(normed, embedding, in_shard_id, col_block=1024, row_block=256):
+    rows, width = normed.shape
+    vocab = embedding.shape[0]
+    col_block = min(col_block, vocab)
+    row_block = min(row_block, rows)
+    stat = jax.ShapeDtypeStruct((rows, 1), jnp.float32)
+    resident = pl.BlockSpec((rows, 1), lambda j: (0, 0))
+    outs = pl.pallas_call(
+        functools.partial(stats_kernel, row_block),
+        grid=(vocab // col_block,),
+        in_specs=[
+            pl.BlockSpec((rows, width), lambda j: (0, 0)),
+            pl.BlockSpec((col_block, width), lambda j: (j, 0)),
+            pl.BlockSpec((rows, 1), lambda j: (0, 0)),
+        ],
+        out_specs=[resident] * 4,
+        out_shape=[stat] * 4,
+        compiler_params=pltpu.CompilerParams(
+            dimension_semantics=("arbitrary",), vmem_limit_bytes=48 * 1024 * 1024
+        ),
+        cost_estimate=pl.CostEstimate(
+            flops=2 * rows * vocab * width,
+            transcendentals=rows * vocab,
+            bytes_accessed=rows * width * 2 + vocab * width * 2 + rows * 20,
+        ),
+    )(normed, embedding, in_shard_id[:, None])
+    return jnp.stack([o[:, 0] for o in outs])
+
+
 def body(final_states, norm_gain, embedding, targets, deal):
     owners = lax.axis_size("req")
     own_rows = final_states.shape[0]
     shard_cols = embedding.shape[0]
     vocab_start = lax.axis_index("tp") * shard_cols
     member = (deal[:, None] // own_rows == jnp.arange(owners, dtype=jnp.int32)[None, :])
-    counts = lax.psum(jnp.sum(member.astype(jnp.int32), axis=0), "req")
-    live_count = counts[lax.axis_index("req")]
+    counts = lax.all_gather(jnp.sum(member.astype(jnp.int32), axis=0), "req")
+    live_count = jnp.sum(counts[:, lax.axis_index("req")])
     live = jnp.arange(own_rows, dtype=jnp.int32) < live_count
 
-    in_shard_id = targets - vocab_start
-    block = 512 if own_rows % 512 == 0 else own_rows
-    parts = []
-    for b in range(own_rows // block):
-        rows = slice(b * block, (b + 1) * block)
-        normed = rms_normed(final_states[rows], norm_gain)
-        parts.append(shard_stats(normed, embedding, in_shard_id[rows]))
-    stats = jnp.concatenate(parts, axis=1)
+    normed = rms_normed(final_states, norm_gain)
+    stats = shard_stats(normed, embedding, targets - vocab_start)
     gathered = lax.all_gather(stats, "tp")
     peaks = gathered[:, 0]
     row_peak = jnp.max(peaks, axis=0)

time: 134 us -> 123 us (0.918)
  Pallas kernels: 0 us -> 77.4 us
  matrix products: 65.8 us -> 0 us
  other arithmetic: 43.9 us -> 16.7 us
  local copies, waits for them, and re-layouts: 0.59 us -> 3.95 us
    pallas_call x0 -> x1, Pallas kernels: none -> 77.4 us  [shard_stats(): pl.pallas_call(functools.partial(stats_kernel, row_block), grid=(vocab //...]
    dot_general x4 -> x0, matrix products: 65.8 us -> none  [shard_stats(): lax.dot_general(normed, embedding, (((1,), (1,)), ((), ())), preferred_el...]
    reduce_sum x5 -> x2, other arithmetic: 37 us -> 0.84 us  [the longest x1 0.71 us: body(): live_count = jnp.sum(counts[:, lax.axis_index('req')])]
    psum x1 -> x0, blocking collectives: 9.47 us -> none  [body(): counts = lax.psum(jnp.sum(member.astype(jnp.int32), axis=0), 'req')]
    unnamed x0 -> x1, blocking collectives: none -> 9.47 us
    convert_element_type x0 -> x1, other arithmetic: none -> 5.19 us  [rms_normed(): (states * lax.rsqrt(mean_square + 1e-06) * norm_gain[None, :]).astype(jnp...]
    pallas_call x0 -> x4, other arithmetic: none -> 3.82 us  [shard_stats(): pl.pallas_call(functools.partial(stats_kernel, row_block), grid=(vocab //...]
    unnamed x2 -> x9, local copies, waits for them, and re-layouts: 0.01 us -> 3.51 us
where the time goes in v2:
time: 123 us
  Pallas kernels  77.4 us (63%)
  blocking collectives  23.1 us (19%)
  other arithmetic  16.7 us (14%)
  local copies, waits for them, and re-layouts  3.95 us (3%)
  between operations  1.38 us (1%)
    pallas_call x1, Pallas kernels, shard_stats(): pl.pallas_call(functools.partial(stats_kernel, row_block), grid=(vocab //...  77.4 us
    all_gather x1, blocking collectives, body(): gathered = lax.all_gather(stats, 'tp')  13.6 us
    unnamed x1, blocking collectives  9.47 us
    convert_element_type x1, other arithmetic, rms_normed(): (states * lax.rsqrt(mean_square + 1e-06) * norm_gain[None, :]).astype(jnp...  5.19 us
    reduce_sum x1, other arithmetic, rms_normed(): mean_square = jnp.mean(states * states, axis=1, keepdims=True)  4 us
    pallas_call x4, other arithmetic, shard_stats(): pl.pallas_call(functools.partial(stats_kernel, row_block), grid=(vocab //...  3.82 us
    unnamed x9, local copies, waits for them, and re-layouts  3.51 us

profile of v2, /device:TPU:0, one launch (start us, length us, event | category | flops | bytes accessed | tf_op | source)
XLA Modules:
  0.0 122.5 jit_solution(1953763514871233533)
XLA Ops:
  0.6 0.0 copy-start.2
  0.6 1.2 %dynamic-slice = u32[1]{0:T(128)} dynamic-slice(u32[32]{0:T(128)} %constant.41, u32[]{:T(128)S(6)} %add.23), dynamic_slice_sizes={1} | dynamic-slice | bytes 12
  2.5 0.7 add_select_fusion
  3.2 0.1 convert_reduce_fusion
  3.4 0.2 dynamic-update-slice
  3.6 0.1 reshape.33
  3.7 9.5 %all-reduce.1 = s32[8,8]{1,0:T(8,128)S(1)} all-reduce(s32[8,8]{1,0:T(8,128)S(1)} %reshape.33), channel_id=2, replica_groups=mesh['req'=8,'tp'=4] {'req'}, use_global_device_ids=true, to_apply=%add | all-reduce | flops 64 | bytes 512
  13.2 0.7 dynamic-slice_reduce_fusion
  13.9 0.7 broadcast_subtract_fusion
  14.6 4.0 %multiply_reduce_fusion = f32[2048]{0:T(1024)S(1)} fusion(f32[2048,1024]{1,0:T(8,128)} %param.5), kind=kLoop, calls=%fused_computation.1 | loop fusion | flops 4192256 | bytes 8396800 | tf_op jit(solution)/shard_map/reduce_sum | solution.py:12
  18.6 0.4 copy.15.ids_ref
  18.9 0.0 copy-done.2
  19.0 5.2 %multiply_convert_fusion.normed_ref = bf16[2048,1024]{1,0:T(8,128)(2,1)} fusion(f32[2048,1024]{1,0:T(8,128)} %param.5, f32[1024]{0:T(1024)S(1)} %copy-done.2, f32[2048]{0:T(1024)S(1)} %add_rsqrt_fusion), kind=kLoop, calls=%fused_computation | loop fusion | flops 6291456 | bytes 12595200 | tf_op jit(solution)/shard_map/convert_element_type | solution.py:13
  24.1 77.4 %shard_map.68 = (f32[2048,1]{1,0:T(8,128)S(1)}, f32[2048,1]{1,0:T(8,128)S(1)}, f32[2048,1]{1,0:T(8,128)S(1)}, f32[2048,1]{1,0:T(8,128)S(1)}) custom-call(bf16[2048,1024]{1,0:T(8,128)(2,1)} %multiply_convert_fusion.normed_ref, bf16[8192,1024]{1,0:T(8,128)(2,1)} %emb_ref.1, s32[2048,1]{1,0:T(8,128)S(1)} %copy.15.ids_ref), custom_call_target="tpu_custom_call" | custom-call | flops 34359738368 | bytes 21012480 | tf_op jit(solution)/shard_map/pallas_call | solution.py:74
  101.6 1.0 copy-done
  102.6 1.0 copy-done.1
  103.6 1.6 %reduce.3 = f32[2048]{0:T(1024)S(1)} reduce(f32[2048,1]{1,0:T(8,128)} %copy-done.1, f32[]{:T(128)} %constant.45), dimensions={1}, to_apply=%get-tuple-element.6.reduce_sub_computation | reduce | bytes 16388 | tf_op jit(solution)/shard_map/pallas_call | solution.py:74
  105.2 1.6 %reduce.4 = f32[2048]{0:T(1024)S(1)} reduce(f32[2048,1]{1,0:T(8,128)} %copy-done, f32[]{:T(128)} %constant.45), dimensions={1}, to_apply=%get-tuple-element.7.reduce_sub_computation | reduce | bytes 16388 | tf_op jit(solution)/shard_map/pallas_call | solution.py:74
  106.7 0.3 reduce.5
  107.1 0.3 reduce.6
  107.5 13.6 %all-gather.2 = f32[4,4,2048]{2,1,0:T(4,128)S(1)} all-gather(f32[1,4,2048]{2,1,0:T(4,128)S(1)} %maximum_bitcast_fusion), channel_id=3, replica_groups=mesh['req'=8,'tp'=4] {'tp'}, dimensions={0}, use_global_device_ids=true | all-gather | bytes 163840 | tf_op jit(solution)/shard_map/all_gather | solution.py:108
  121.1 0.1 fusion.7
  121.2 0.1 fusion.1
  121.3 1.2 %subtract_select_fusion = (f32[2048]{0:T(1024)}, f32[2048]{0:T(1024)}) fusion(f32[2048]{0:T(1024)S(1)} %get-tuple-element.12, f32[2048]{0:T(1024)S(1)} %get-tuple-element.13, f32[2048]{0:T(1024)S(1)} %get-tuple-element.18, s32[]{:T(128)} %dynamic-slice_reduce_fusion, f32[2048]{0:T(1024)S(1)} %get-tuple-element.17), kind=kLoop, calls=%fused_computation.14 | loop fusion | flops 14336 | bytes 49156 | tf_op jit(solution)/shard_map/jit(_where)/select_n | solution.py:118
  (5 shorter events, 0.0 us)
Async XLA Ops:
  0.6 18.3 %copy-start.2 = (f32[1024]{0:T(1024)S(1)}, f32[1024]{0:T(1024)}, u32[]{:S(2)}) copy-start(f32[1024]{0:T(1024)} %param.6) | copy-start | bytes 12292
  101.6 1.0 copy-start
  102.5 1.0 copy-start.1

commit v3 on v2

--- a/solution.py
+++ b/solution.py
@@ -38,26 +38,27 @@
         chosen_ref[...] = jnp.zeros(chosen_ref.shape, jnp.float32)
 
     table = emb_ref[...]
-    cols = lax.broadcasted_iota(jnp.int32, (row_block, col_block), 1)
+    vocab_ids = lax.broadcasted_iota(jnp.int32, (col_block, row_block), 0)
 
     def chunk(r, carry):
-        rows = pl.ds(pl.multiple_of(r * row_block, row_block), row_block)
+        start = pl.multiple_of(r * row_block, row_block)
+        rows = pl.ds(start, row_block)
         logits = lax.dot_general(
-            normed_ref[rows, :], table, (((1,), (1,)), ((), ())),
+            table, normed_ref[rows, :], (((1,), (1,)), ((), ())),
             preferred_element_type=jnp.float32,
         )
-        old_peak = peak_ref[rows, :]
-        new_peak = jnp.maximum(old_peak, jnp.max(logits, axis=1, keepdims=True))
+        old_peak = peak_ref[:, rows]
+        new_peak = jnp.maximum(old_peak, jnp.max(logits, axis=0, keepdims=True))
         weights = jnp.exp(logits - new_peak)
         scale = jnp.exp(old_peak - new_peak)
-        total_ref[rows, :] = total_ref[rows, :] * scale + jnp.sum(weights, axis=1, keepdims=True)
-        moment_ref[rows, :] = moment_ref[rows, :] * scale + jnp.sum(
-            weights * logits, axis=1, keepdims=True
+        total_ref[:, rows] = total_ref[:, rows] * scale + jnp.sum(weights, axis=0, keepdims=True)
+        moment_ref[:, rows] = moment_ref[:, rows] * scale + jnp.sum(
+            weights * logits, axis=0, keepdims=True
         )
-        peak_ref[rows, :] = new_peak
-        local_id = ids_ref[rows, :] - j * col_block
-        chosen_ref[rows, :] = chosen_ref[rows, :] + jnp.sum(
-            jnp.where(cols == local_id, logits, 0.0), axis=1, keepdims=True
+        peak_ref[:, rows] = new_peak
+        local_id = ids_ref[:, rows] - j * col_block
+        chosen_ref[:, rows] = chosen_ref[:, rows] + jnp.sum(
+            jnp.where(vocab_ids == local_id, logits, 0.0), axis=0, keepdims=True
         )
         return carry
 
@@ -69,15 +70,15 @@
     vocab = embedding.shape[0]
     col_block = min(col_block, vocab)
     row_block = min(row_block, rows)
-    stat = jax.ShapeDtypeStruct((rows, 1), jnp.float32)
-    resident = pl.BlockSpec((rows, 1), lambda j: (0, 0))
+    stat = jax.ShapeDtypeStruct((1, rows), jnp.float32)
+    resident = pl.BlockSpec((1, rows), lambda j: (0, 0))
     outs = pl.pallas_call(
         functools.partial(stats_kernel, row_block),
         grid=(vocab // col_block,),
         in_specs=[
             pl.BlockSpec((rows, width), lambda j: (0, 0)),
             pl.BlockSpec((col_block, width), lambda j: (j, 0)),
-            pl.BlockSpec((rows, 1), lambda j: (0, 0)),
+            pl.BlockSpec((1, rows), lambda j: (0, 0)),
         ],
         out_specs=[resident] * 4,
         out_shape=[stat] * 4,
@@ -89,8 +90,8 @@
             transcendentals=rows * vocab,
             bytes_accessed=rows * width * 2 + vocab * width * 2 + rows * 20,
         ),
-    )(normed, embedding, in_shard_id[:, None])
-    return jnp.stack([o[:, 0] for o in outs])
+    )(normed, embedding, in_shard_id[None, :])
+    return jnp.concatenate(outs, axis=0)
 
 
 def body(final_states, norm_gain, embedding, targets, deal):

time: 123 us -> 108 us (0.88)
  other arithmetic: 16.7 us -> 9.33 us
  Pallas kernels: 77.4 us -> 72.9 us
  local copies, waits for them, and re-layouts: 3.95 us -> 1.57 us
    pallas_call x1, Pallas kernels: 77.4 us -> 72.9 us  [shard_stats(): pl.pallas_call(functools.partial(stats_kernel, row_block), grid=(vocab //...]
    convert_element_type x1, other arithmetic: 5.19 us -> 0.88 us  [rms_normed(): (states * lax.rsqrt(mean_square + 1e-06) * norm_gain[None, :]).astype(jnp...]
    pallas_call x4 -> x0, other arithmetic: 3.82 us -> none  [shard_stats(): pl.pallas_call(functools.partial(stats_kernel, row_block), grid=(vocab //...]
    unnamed x9 -> x7, local copies, waits for them, and re-layouts: 3.51 us -> 1.49 us
where the time goes in v3:
time: 108 us
  Pallas kernels  72.9 us (68%)
  blocking collectives  23.1 us (21%)
  other arithmetic  9.33 us (9%)
  local copies, waits for them, and re-layouts  1.57 us (1%)
  between operations  1.36 us (1%)
    pallas_call x1, Pallas kernels, shard_stats(): pl.pallas_call(functools.partial(stats_kernel, row_block), grid=(vocab //...  72.9 us
    all_gather x1, blocking collectives, body(): gathered = lax.all_gather(stats, 'tp')  13.6 us
    unnamed x1, blocking collectives  9.47 us
    reduce_sum x1, other arithmetic, rms_normed(): mean_square = jnp.mean(states * states, axis=1, keepdims=True)  4.27 us

profile of v3, /device:TPU:0, one launch (start us, length us, event | category | flops | bytes accessed | tf_op | source)
XLA Modules:
  0.0 108.2 jit_solution(16829602016190048267)
XLA Ops:
  0.6 0.0 copy-start.1
  0.6 1.2 %dynamic-slice = u32[1]{0:T(128)} dynamic-slice(u32[32]{0:T(128)} %constant.41, u32[]{:T(128)S(6)} %add.23), dynamic_slice_sizes={1} | dynamic-slice | bytes 12
  2.5 0.7 add_select_fusion
  3.2 0.1 convert_reduce_fusion
  3.4 0.2 dynamic-update-slice
  3.6 0.1 reshape.33
  3.7 9.5 %all-reduce.1 = s32[8,8]{1,0:T(8,128)S(1)} all-reduce(s32[8,8]{1,0:T(8,128)S(1)} %reshape.33), channel_id=2, replica_groups=mesh['req'=8,'tp'=4] {'req'}, use_global_device_ids=true, to_apply=%add | all-reduce | flops 64 | bytes 512
  13.2 0.0 copy-start
  13.2 0.8 dynamic-slice_reduce_fusion
  13.9 1.0 broadcast_subtract_fusion
  15.0 4.3 %multiply_reduce_fusion = f32[2048]{0:T(1024)S(1)} fusion(f32[2048,1024]{1,0:T(8,128)} %param.5), kind=kLoop, calls=%fused_computation.1 | loop fusion | flops 4192256 | bytes 8396800 | tf_op jit(solution)/shard_map/reduce_sum | solution.py:12
  19.2 0.0 copy-done.1
  19.3 0.0 copy-done
  19.3 0.9 multiply_convert_fusion.normed_ref
  20.2 72.9 %shard_map.68 = (f32[1,2048]{1,0:T(1,128)S(1)}, f32[1,2048]{1,0:T(1,128)S(1)}, f32[1,2048]{1,0:T(1,128)S(1)}, f32[1,2048]{1,0:T(1,128)S(1)}) custom-call(bf16[2048,1024]{1,0:T(8,128)(2,1)S(1)} %multiply_convert_fusion.normed_ref, bf16[8192,1024]{1,0:T(8,128)(2,1)} %emb_ref.1, s32[1,2048]{1,0:T(1,128)S(1)} %bitcast.24), custom_call_target="tpu_custom_call" | custom-call | flops 34359738368 | bytes 21012480 | tf_op jit(solution)/shard_map/pallas_call | solution.py:75
  93.1 13.6 %all-gather.2 = f32[4,4,2048]{2,1,0:T(4,128)S(1)} all-gather(f32[1,4,2048]{2,1,0:T(4,128)S(1)} %maximum_bitcast_fusion), channel_id=3, replica_groups=mesh['req'=8,'tp'=4] {'tp'}, dimensions={0}, use_global_device_ids=true | all-gather | bytes 163840 | tf_op jit(solution)/shard_map/all_gather | solution.py:109
  106.7 0.1 fusion.7
  106.8 0.1 fusion.1
  106.9 1.3 %subtract_select_fusion = (f32[2048]{0:T(1024)}, f32[2048]{0:T(1024)}) fusion(f32[2048]{0:T(1024)S(1)} %get-tuple-element.12, f32[2048]{0:T(1024)S(1)} %get-tuple-element.13, f32[2048]{0:T(1024)S(1)} %get-tuple-element.18, s32[]{:T(128)} %dynamic-slice_reduce_fusion, f32[2048]{0:T(1024)S(1)} %get-tuple-element.17), kind=kLoop, calls=%fused_computation.14 | loop fusion | flops 14336 | bytes 49156 | tf_op jit(solution)/shard_map/jit(_where)/select_n | solution.py:119
  (3 shorter events, 0.0 us)
Async XLA Ops:
  0.6 18.6 %copy-start.1 = (f32[1024]{0:T(1024)S(1)}, f32[1024]{0:T(1024)}, u32[]{:S(2)}) copy-start(f32[1024]{0:T(1024)} %param.6) | copy-start | bytes 12292
  13.2 6.1 %copy-start = (f32[2048,1024]{1,0:T(8,128)S(1)}, f32[2048,1024]{1,0:T(8,128)}, u32[]{:S(2)}) copy-start(f32[2048,1024]{1,0:T(8,128)} %param.5) | copy-start | bytes 25165828

commit v4 on v3

--- a/solution.py
+++ b/solution.py
@@ -94,19 +94,15 @@
     return jnp.concatenate(outs, axis=0)
 
 
-def body(final_states, norm_gain, embedding, targets, deal):
-    owners = lax.axis_size("req")
-    own_rows = final_states.shape[0]
-    shard_cols = embedding.shape[0]
-    vocab_start = lax.axis_index("tp") * shard_cols
-    member = (deal[:, None] // own_rows == jnp.arange(owners, dtype=jnp.int32)[None, :])
-    counts = lax.all_gather(jnp.sum(member.astype(jnp.int32), axis=0), "req")
-    live_count = jnp.sum(counts[:, lax.axis_index("req")])
-    live = jnp.arange(own_rows, dtype=jnp.int32) < live_count
-
-    normed = rms_normed(final_states, norm_gain)
-    stats = shard_stats(normed, embedding, targets - vocab_start)
-    gathered = lax.all_gather(stats, "tp")
+def combine_over_tp(stats):
+    group = lax.axis_size("tp")
+    me = lax.axis_index("tp")
+    pieces = [stats]
+    for shift in range(1, group):
+        pieces.append(
+            lax.ppermute(stats, "tp", [(d, (d + shift) % group) for d in range(group)])
+        )
+    gathered = jnp.stack(pieces)
     peaks = gathered[:, 0]
     row_peak = jnp.max(peaks, axis=0)
     scale = jnp.exp(peaks - row_peak[None, :])
@@ -115,8 +111,44 @@
     chosen = jnp.sum(gathered[:, 3], axis=0)
     log_total = row_peak + jnp.log(exp_total)
     expected = moment / exp_total
-    logprob = jnp.where(live, chosen - log_total, 0.0)
-    entropy = jnp.where(live, log_total - expected, 0.0)
+    return chosen - log_total, log_total - expected
+
+
+def live_count_of_owner(deal, own_rows):
+    owners = lax.axis_size("req")
+    me = lax.axis_index("req")
+    member = (deal[:, None] // own_rows == jnp.arange(owners, dtype=jnp.int32)[None, :])
+    counts = jnp.sum(member.astype(jnp.int32), axis=0)
+    received = [lax.dynamic_slice(counts, (me,), (1,))]
+    for shift in range(1, owners):
+        sent = lax.dynamic_slice(counts, ((me + shift) % owners,), (1,))
+        received.append(
+            lax.ppermute(sent, "req", [(d, (d + shift) % owners) for d in range(owners)])
+        )
+    return jnp.sum(jnp.concatenate(received))
+
+
+def body(final_states, norm_gain, embedding, targets, deal):
+    own_rows = final_states.shape[0]
+    shard_cols = embedding.shape[0]
+    vocab_start = lax.axis_index("tp") * shard_cols
+    live_count = live_count_of_owner(deal, own_rows)
+
+    normed = rms_normed(final_states, norm_gain)
+    in_shard_id = targets - vocab_start
+    half = own_rows // 2 if own_rows % 512 == 0 else own_rows
+    logprob_parts, entropy_parts = [], []
+    for start in range(0, own_rows, half):
+        rows_normed = normed[start:start + half]
+        if start > 0:
+            rows_normed, live_count = lax.optimization_barrier((rows_normed, live_count))
+        stats = shard_stats(rows_normed, embedding, in_shard_id[start:start + half])
+        logprob_part, entropy_part = combine_over_tp(stats)
+        logprob_parts.append(logprob_part)
+        entropy_parts.append(entropy_part)
+    live = jnp.arange(own_rows, dtype=jnp.int32) < live_count
+    logprob = jnp.where(live, jnp.concatenate(logprob_parts), 0.0)
+    entropy = jnp.where(live, jnp.concatenate(entropy_parts), 0.0)
     return (logprob, entropy)
 
 

time: 108 us -> 119 us (1.10)
  blocking collectives: 23.1 us -> 0 us
  starting transfers between devices: 0 us -> 16.7 us
  waiting for transfers between devices: 0 us -> 8.34 us
  between operations: 1.36 us -> 5.86 us
  local copies, waits for them, and re-layouts: 1.57 us -> 5.68 us
  other arithmetic: 9.33 us -> 6.08 us
  Pallas kernels: 72.9 us -> 75.7 us
    ppermute x0 -> x13, starting transfers between devices: none -> 16.7 us  [the longest x6 10.1 us: combine_over_tp(): lax.ppermute(stats, 'tp', [(d, (d + shift) % group) for d in range(group)])]
    all_gather x1 -> x0, blocking collectives: 13.6 us -> none  [body(): gathered = lax.all_gather(stats, 'tp')]
    unnamed x1 -> x0, blocking collectives: 9.47 us -> none
    ppermute x0 -> x13, waiting for transfers between devices: none -> 8.34 us  [the longest x6 5.36 us: combine_over_tp(): lax.ppermute(stats, 'tp', [(d, (d + shift) % group) for d in range(group)])]
    pallas_call x1 -> x2, Pallas kernels: 72.9 us -> 75.7 us  [shard_stats(): pl.pallas_call(functools.partial(stats_kernel, row_block), grid=(vocab //...]
    slice x0 -> x2, local copies, waits for them, and re-layouts: none -> 1.79 us  [the longest x1 1.78 us: body(): rows_normed = normed[start:start + half]]
    unnamed x7 -> x10, local copies, waits for them, and re-layouts: 1.49 us -> 3.18 us
    select_n x2, other arithmetic: 2 us -> 0.62 us  [the longest x1 0.61 us: body(): logprob = jnp.where(live, jnp.concatenate(logprob_parts), 0.0)]
  transfers between devices with their start and end apart: 0 -> 13, of which waited for: 0 -> 5; matrix products, arithmetic and copies ran while one was open for 0% -> 1% of each run, Pallas kernels for 0% -> 32%
where the time goes in v4:
time: 119 us; the launch traced here: 118 us
  Pallas kernels  75.7 us (64%)
  starting transfers between devices  16.7 us (14%)
  waiting for transfers between devices  8.34 us (7%)
  other arithmetic  6.08 us (5%)
  between operations  5.86 us (5%)
  local copies, waits for them, and re-layouts  5.68 us (5%)
    pallas_call x2, Pallas kernels, shard_stats(): pl.pallas_call(functools.partial(stats_kernel, row_block), grid=(vocab //...  75.7 us
    ppermute x6, starting transfers between devices, combine_over_tp(): lax.ppermute(stats, 'tp', [(d, (d + shift) % group) for d in range(group)])  10.1 us
    ppermute x7, starting transfers between devices, live_count_of_owner(): lax.ppermute(sent, 'req', [(d, (d + shift) % owners) for d in range(owner...  6.59 us
    ppermute x6, waiting for transfers between devices, combine_over_tp(): lax.ppermute(stats, 'tp', [(d, (d + shift) % group) for d in range(group)])  5.36 us
    reduce_sum x1, other arithmetic, rms_normed(): mean_square = jnp.mean(states * states, axis=1, keepdims=True)  4.15 us
    unnamed x10, local copies, waits for them, and re-layouts  3.18 us
    ppermute x7, waiting for transfers between devices, live_count_of_owner(): lax.ppermute(sent, 'req', [(d, (d + shift) % owners) for d in range(owner...  2.98 us
  transfers between devices with their start and end apart: 13, of which 5 were waited for; matrix products, arithmetic and copies ran while one was open for 1% of the time, Pallas kernels for 32%

profile of v4, /device:TPU:0, one launch (start us, length us, event | category | flops | bytes accessed | tf_op | source)
XLA Modules:
  0.0 118.4 jit_solution(1313323822036394499)
XLA Ops:
  0.7 4.1 %multiply_reduce_fusion = f32[2048]{0:T(1024)S(1)} fusion(f32[2048,1024]{1,0:T(8,128)} %param.5), kind=kLoop, calls=%fused_computation.1 | loop fusion | flops 4192256 | bytes 8396800 | tf_op jit(solution)/shard_map/reduce_sum | solution.py:12
  4.8 1.6 %copy-done.1 = f32[2048,1024]{1,0:T(8,128)S(1)} copy-done((f32[2048,1024]{1,0:T(8,128)S(1)}, f32[2048,1024]{1,0:T(8,128)}, u32[]{:S(2)}) %copy-start.1) | copy-done | bytes 8388632
  6.4 0.9 multiply_convert_fusion
  7.3 1.8 %fusion.16 = (bf16[1024,1024]{1,0:T(8,128)(2,1)}, bf16[1024,1024]{1,0:T(8,128)(2,1)S(1)}) fusion(bf16[2048,1024]{1,0:T(8,128)(2,1)S(1)} %multiply_convert_fusion), kind=kLoop, calls=%fused_computation.48 | loop fusion | bytes 8388608 | tf_op jit(solution)/shard_map/slice | solution.py:142
  9.1 1.6 %copy-done = bf16[1024,1024]{1,0:T(8,128)(2,1)S(1)} copy-done((bf16[1024,1024]{1,0:T(8,128)(2,1)S(1)}, bf16[1024,1024]{1,0:T(8,128)(2,1)}, u32[]{:S(2)}) %copy-start) | copy-done | bytes 2097176
  10.7 37.8 %shard_map.68 = (f32[1,1024]{1,0:T(1,128)S(1)}, f32[1,1024]{1,0:T(1,128)S(1)}, f32[1,1024]{1,0:T(1,128)S(1)}, f32[1,1024]{1,0:T(1,128)S(1)}) custom-call(bf16[1024,1024]{1,0:T(8,128)(2,1)S(1)} %copy-done, bf16[8192,1024]{1,0:T(8,128)(2,1)} %emb_ref.3, s32[1,1024]{1,0:T(1,128)S(1)} %bitcast.54), custom_call_target="tpu_custom_call" | custom-call | flops 17179869184 | bytes 18894848 | tf_op jit(solution)/shard_map/pallas_call | solution.py:75
  48.5 5.1 %collective-permute-start.9 = (f32[4,1024]{1,0:T(4,128)S(1)}, f32[4,1024]{1,0:T(4,128)S(1)}, u32[]{:S(2)}, u32[]{:S(2)}) collective-permute-start(f32[4,1024]{1,0:T(4,128)S(1)} %get-tuple-element.43), channel_id=1, source_target_pairs={{0,3},{1,0},{2,1},{3,2},{4,7},{5,4},{6,5},{7,6},{8,11},{9,8},{10,9... | collective-permute-start | bytes 49160 | tf_op jit(solution)/shard_map/ppermute | solution.py:103
  53.7 1.0 collective-permute-start.7
  54.7 0.1 convert_reduce_fusion
  54.8 0.7 fusion.20
  55.5 1.5 %collective-permute-start.1 = (s32[1]{0:T(128)}, s32[1]{0:T(128)}, u32[]{:S(2)}, u32[]{:S(2)}) collective-permute-start(s32[1]{0:T(128)} %get-tuple-element.57), channel_id=1, source_target_pairs={{0,8},{4,12},{8,16},{12,20},{16,24},{20,28},{24,0},{28,4},{1,9},{5... | collective-permute-start | bytes 20 | tf_op jit(solution)/shard_map/ppermute | solution.py:126
  57.1 2.5 %collective-permute-done = s32[1]{0:T(128)} collective-permute-done((s32[1]{0:T(128)}, s32[1]{0:T(128)}, u32[]{:S(2)}, u32[]{:S(2)}) %collective-permute-start) | collective-permute-done | bytes 36 | tf_op jit(solution)/shard_map/ppermute | solution.py:126
  60.8 1.6 %collective-permute-start.3 = (s32[1]{0:T(128)}, s32[1]{0:T(128)}, u32[]{:S(2)}, u32[]{:S(2)}) collective-permute-start(s32[1]{0:T(128)} %get-tuple-element.55), channel_id=1, source_target_pairs={{0,16},{4,20},{8,24},{12,28},{16,0},{20,4},{24,8},{28,12},{1,17},{... | collective-permute-start | bytes 20 | tf_op jit(solution)/shard_map/ppermute | solution.py:126
  63.0 1.5 %collective-permute-start.4 = (s32[1]{0:T(128)}, s32[1]{0:T(128)}, u32[]{:S(2)}, u32[]{:S(2)}) collective-permute-start(s32[1]{0:T(128)} %get-tuple-element.54), channel_id=1, source_target_pairs={{0,20},{4,24},{8,28},{12,0},{16,4},{20,8},{24,12},{28,16},{1,21},{... | collective-permute-start | bytes 20 | tf_op jit(solution)/shard_map/ppermute | solution.py:126
  65.2 0.9 collective-permute-start.5
  66.8 1.0 collective-permute-start.6
  68.4 0.5 collective-permute-done.5
  70.2 37.8 %shard_map.69 = (f32[1,1024]{1,0:T(1,128)S(1)}, f32[1,1024]{1,0:T(1,128)S(1)}, f32[1,1024]{1,0:T(1,128)S(1)}, f32[1,1024]{1,0:T(1,128)S(1)}) custom-call(bf16[1024,1024]{1,0:T(8,128)(2,1)S(1)} %get-tuple-element.17.normed_ref, bf16[8192,1024]{1,0:T(8,128)(2,1)} %emb_ref.3, s32[1,1024]{1,0:T(1,128)S(1)} %bitcast.53), custom_call_target="tpu_custom_call" | custom-call | flops 17179869184 | bytes 18894848 | tf_op jit(solution)/shard_map/pallas_call | solution.py:75
  108.1 2.9 %collective-permute-start.12 = (f32[4,1024]{1,0:T(4,128)S(1)}, f32[4,1024]{1,0:T(4,128)S(1)}, u32[]{:S(2)}, u32[]{:S(2)}) collective-permute-start(f32[4,1024]{1,0:T(4,128)S(1)} %get-tuple-element.45), channel_id=1, source_target_pairs={{0,3},{1,0},{2,1},{3,2},{4,7},{5,4},{6,5},{7,6},{8,11},{9,8},{10,9... | collective-permute-start | bytes 49160 | tf_op jit(solution)/shard_map/ppermute | solution.py:103
  110.9 1.1 collective-permute-start.11
  112.2 0.1 collective-permute-done.12
  112.4 3.2 %collective-permute-done.11 = f32[4,1024]{1,0:T(4,128)S(1)} collective-permute-done((f32[4,1024]{1,0:T(4,128)S(1)}, f32[4,1024]{1,0:T(4,128)S(1)}, u32[]{:S(2)}, u32[]{:S(2)}) %collective-permute-start.11) | collective-permute-done | bytes 16416 | tf_op jit(solution)/shard_map/ppermute | solution.py:103
  115.6 2.0 %collective-permute-done.10 = f32[4,1024]{1,0:T(4,128)S(1)} collective-permute-done((f32[4,1024]{1,0:T(4,128)S(1)}, f32[4,1024]{1,0:T(4,128)S(1)}, u32[]{:S(2)}, u32[]{:S(2)}) %collective-permute-start.10) | collective-permute-done | bytes 16416 | tf_op jit(solution)/shard_map/ppermute | solution.py:103
  117.7 0.6 maximum_select_fusion
  (34 shorter events, 0.4 us)
Async XLA Ops:
  0.6 5.8 %copy-start.1 = (f32[2048,1024]{1,0:T(8,128)S(1)}, f32[2048,1024]{1,0:T(8,128)}, u32[]{:S(2)}) copy-start(f32[2048,1024]{1,0:T(8,128)} %param.5) | copy-start | bytes 25165828
  0.6 5.8 %copy-start.3 = (f32[1024]{0:T(1024)S(1)}, f32[1024]{0:T(1024)}, u32[]{:S(2)}) copy-start(f32[1024]{0:T(1024)} %param.6) | copy-start | bytes 12292
  6.4 2.7 %copy-start.2 = (s32[2048]{0:T(1024)S(1)}, s32[2048]{0:T(1024)}, u32[]{:S(2)}) copy-start(s32[2048]{0:T(1024)} %param.8) | copy-start | bytes 24580
  9.1 1.6 %copy-start = (bf16[1024,1024]{1,0:T(8,128)(2,1)S(1)}, bf16[1024,1024]{1,0:T(8,128)(2,1)}, u32[]{:S(2)}) copy-start(bf16[1024,1024]{1,0:T(8,128)(2,1)} %get-tuple-element.30.normed_ref) | copy-start | bytes 6291460
  10.7 44.0 %copy-start.4 = (s32[1024]{0:T(1024)S(1)}, s32[1024]{0:T(1024)}, u32[]{:S(2)}) copy-start(s32[1024]{0:T(1024)} %param.9) | copy-start | bytes 12292
  48.5 63.5 %collective-permute-start.9 = (f32[4,1024]{1,0:T(4,128)S(1)}, f32[4,1024]{1,0:T(4,128)S(1)}, u32[]{:S(2)}, u32[]{:S(2)}) collective-permute-start(f32[4,1024]{1,0:T(4,128)S(1)} %get-tuple-element.43), channel_id=1, source_target_pairs={{0,3},{1,0},{2,1},{3,2},{4,7},{5,4},{6,5},{7,6},{8,11},{9,8},{10,9... | collective-permute-start | bytes 49160 | tf_op jit(solution)/shard_map/ppermute | solution.py:103
  53.7 58.4 %collective-permute-start.8 = (f32[4,1024]{1,0:T(4,128)S(1)}, f32[4,1024]{1,0:T(4,128)S(1)}, u32[]{:S(2)}, u32[]{:S(2)}) collective-permute-start(f32[4,1024]{1,0:T(4,128)S(1)} %get-tuple-element.43), channel_id=1, source_target_pairs={{0,2},{1,3},{2,0},{3,1},{4,6},{5,7},{6,4},{7,5},{8,10},{9,11},{10,... | collective-permute-start | bytes 49160 | tf_op jit(solution)/shard_map/ppermute | solution.py:103
  53.7 58.4 %collective-permute-start.7 = (f32[4,1024]{1,0:T(4,128)S(1)}, f32[4,1024]{1,0:T(4,128)S(1)}, u32[]{:S(2)}, u32[]{:S(2)}) collective-permute-start(f32[4,1024]{1,0:T(4,128)S(1)} %get-tuple-element.43), channel_id=1, source_target_pairs={{0,1},{1,2},{2,3},{3,0},{4,5},{5,6},{6,7},{7,4},{8,9},{9,10},{10,1... | collective-permute-start | bytes 49160 | tf_op jit(solution)/shard_map/ppermute | solution.py:103
  55.5 4.0 %collective-permute-start = (s32[1]{0:T(128)}, s32[1]{0:T(128)}, u32[]{:S(2)}, u32[]{:S(2)}) collective-permute-start(s32[1]{0:T(128)} %get-tuple-element.58), channel_id=1, source_target_pairs={{0,4},{4,8},{8,12},{12,16},{16,20},{20,24},{24,28},{28,0},{1,5},{5... | collective-permute-start | bytes 20 | tf_op jit(solution)/shard_map/ppermute | solution.py:126
  55.5 5.3 %collective-permute-start.1 = (s32[1]{0:T(128)}, s32[1]{0:T(128)}, u32[]{:S(2)}, u32[]{:S(2)}) collective-permute-start(s32[1]{0:T(128)} %get-tuple-element.57), channel_id=1, source_target_pairs={{0,8},{4,12},{8,16},{12,20},{16,24},{20,28},{24,0},{28,4},{1,9},{5... | collective-permute-start | bytes 20 | tf_op jit(solution)/shard_map/ppermute | solution.py:126
  59.6 3.4 %collective-permute-start.2 = (s32[1]{0:T(128)}, s32[1]{0:T(128)}, u32[]{:S(2)}, u32[]{:S(2)}) collective-permute-start(s32[1]{0:T(128)} %get-tuple-element.56), channel_id=1, source_target_pairs={{0,12},{4,16},{8,20},{12,24},{16,28},{20,0},{24,4},{28,8},{1,13},{... | collective-permute-start | bytes 20 | tf_op jit(solution)/shard_map/ppermute | solution.py:126
  60.8 4.4 %collective-permute-start.3 = (s32[1]{0:T(128)}, s32[1]{0:T(128)}, u32[]{:S(2)}, u32[]{:S(2)}) collective-permute-start(s32[1]{0:T(128)} %get-tuple-element.55), channel_id=1, source_target_pairs={{0,16},{4,20},{8,24},{12,28},{16,0},{20,4},{24,8},{28,12},{1,17},{... | collective-permute-start | bytes 20 | tf_op jit(solution)/shard_map/ppermute | solution.py:126
  63.0 3.8 %collective-permute-start.4 = (s32[1]{0:T(128)}, s32[1]{0:T(128)}, u32[]{:S(2)}, u32[]{:S(2)}) collective-permute-start(s32[1]{0:T(128)} %get-tuple-element.54), channel_id=1, source_target_pairs={{0,20},{4,24},{8,28},{12,0},{16,4},{20,8},{24,12},{28,16},{1,21},{... | collective-permute-start | bytes 20 | tf_op jit(solution)/shard_map/ppermute | solution.py:126
  65.2 3.7 %collective-permute-start.5 = (s32[1]{0:T(128)}, s32[1]{0:T(128)}, u32[]{:S(2)}, u32[]{:S(2)}) collective-permute-start(s32[1]{0:T(128)} %get-tuple-element.53), channel_id=1, source_target_pairs={{0,24},{4,28},{8,0},{12,4},{16,8},{20,12},{24,16},{28,20},{1,25},{... | collective-permute-start | bytes 20 | tf_op jit(solution)/shard_map/ppermute | solution.py:126
  66.8 2.8 %collective-permute-start.6 = (s32[1]{0:T(128)}, s32[1]{0:T(128)}, u32[]{:S(2)}, u32[]{:S(2)}) collective-permute-start(s32[1]{0:T(128)} %get-tuple-element.52), channel_id=1, source_target_pairs={{0,28},{4,0},{8,4},{12,8},{16,12},{20,16},{24,20},{28,24},{1,29},{... | collective-permute-start | bytes 20 | tf_op jit(solution)/shard_map/ppermute | solution.py:126
  108.1 4.3 %collective-permute-start.12 = (f32[4,1024]{1,0:T(4,128)S(1)}, f32[4,1024]{1,0:T(4,128)S(1)}, u32[]{:S(2)}, u32[]{:S(2)}) collective-permute-start(f32[4,1024]{1,0:T(4,128)S(1)} %get-tuple-element.45), channel_id=1, source_target_pairs={{0,3},{1,0},{2,1},{3,2},{4,7},{5,4},{6,5},{7,6},{8,11},{9,8},{10,9... | collective-permute-start | bytes 49160 | tf_op jit(solution)/shard_map/ppermute | solution.py:103
  110.9 4.6 %collective-permute-start.11 = (f32[4,1024]{1,0:T(4,128)S(1)}, f32[4,1024]{1,0:T(4,128)S(1)}, u32[]{:S(2)}, u32[]{:S(2)}) collective-permute-start(f32[4,1024]{1,0:T(4,128)S(1)} %get-tuple-element.45), channel_id=1, source_target_pairs={{0,2},{1,3},{2,0},{3,1},{4,6},{5,7},{6,4},{7,5},{8,10},{9,11},{10,... | collective-permute-start | bytes 49160 | tf_op jit(solution)/shard_map/ppermute | solution.py:103
  112.0 5.5 %collective-permute-start.10 = (f32[4,1024]{1,0:T(4,128)S(1)}, f32[4,1024]{1,0:T(4,128)S(1)}, u32[]{:S(2)}, u32[]{:S(2)}) collective-permute-start(f32[4,1024]{1,0:T(4,128)S(1)} %get-tuple-element.45), channel_id=1, source_target_pairs={{0,1},{1,2},{2,3},{3,0},{4,5},{5,6},{6,7},{7,4},{8,9},{9,10},{10,1... | collective-permute-start | bytes 49160 | tf_op jit(solution)/shard_map/ppermute | solution.py:103

commit v5 on v3

--- a/solution.py
+++ b/solution.py
@@ -62,7 +62,7 @@
         )
         return carry
 
-    lax.fori_loop(0, normed_ref.shape[0] // row_block, chunk, 0)
+    lax.fori_loop(0, normed_ref.shape[0] // row_block, chunk, 0, unroll=True)
 
 
 def shard_stats(normed, embedding, in_shard_id, col_block=1024, row_block=256):

time: 108 us -> 92.6 us (0.86)
  Pallas kernels: 72.9 us -> 57 us
    pallas_call x1, Pallas kernels: 72.9 us -> 57 us  [shard_stats(): pl.pallas_call(functools.partial(stats_kernel, row_block), grid=(vocab //...]
where the time goes in v5:
time: 92.6 us; the launch traced here: 92.3 us
  Pallas kernels  57 us (62%)
  blocking collectives  23.1 us (25%)
  other arithmetic  9.33 us (10%)
  local copies, waits for them, and re-layouts  1.57 us (2%)
  between operations  1.36 us (1%)
    pallas_call x1, Pallas kernels, shard_stats(): pl.pallas_call(functools.partial(stats_kernel, row_block), grid=(vocab //...  57 us
    all_gather x1, blocking collectives, body(): gathered = lax.all_gather(stats, 'tp')  13.6 us
    unnamed x1, blocking collectives  9.47 us
    reduce_sum x1, other arithmetic, rms_normed(): mean_square = jnp.mean(states * states, axis=1, keepdims=True)  4.27 us

profile of v5, /device:TPU:0, one launch (start us, length us, event | category | flops | bytes accessed | tf_op | source)
XLA Modules:
  0.0 92.3 jit_solution(16283468362542602964)
XLA Ops:
  0.6 0.0 copy-start.1
  0.6 1.2 %dynamic-slice = u32[1]{0:T(128)} dynamic-slice(u32[32]{0:T(128)} %constant.41, u32[]{:T(128)S(6)} %add.23), dynamic_slice_sizes={1} | dynamic-slice | bytes 12
  2.5 0.7 add_select_fusion
  3.2 0.1 convert_reduce_fusion
  3.4 0.2 dynamic-update-slice
  3.6 0.1 reshape.33
  3.7 9.5 %all-reduce.1 = s32[8,8]{1,0:T(8,128)S(1)} all-reduce(s32[8,8]{1,0:T(8,128)S(1)} %reshape.33), channel_id=2, replica_groups=mesh['req'=8,'tp'=4] {'req'}, use_global_device_ids=true, to_apply=%add | all-reduce | flops 64 | bytes 512
  13.2 0.0 copy-start
  13.2 0.8 dynamic-slice_reduce_fusion
  13.9 1.0 %broadcast_subtract_fusion = s32[2048]{0:T(1024)S(1)} fusion(s32[2048]{0:T(1024)} %param.8, s32[]{:T(128)S(6)} %mul.33), kind=kLoop, calls=%fused_computation.24 | loop fusion | flops 2048 | bytes 16388 | tf_op jit(solution)/shard_map/sub | solution.py:108
  15.0 4.3 %multiply_reduce_fusion = f32[2048]{0:T(1024)S(1)} fusion(f32[2048,1024]{1,0:T(8,128)} %param.5), kind=kLoop, calls=%fused_computation.1 | loop fusion | flops 4192256 | bytes 8396800 | tf_op jit(solution)/shard_map/reduce_sum | solution.py:12
  19.2 0.0 copy-done.1
  19.3 0.0 copy-done
  19.3 0.9 multiply_convert_fusion.normed_ref
  20.2 57.0 %shard_map.68 = (f32[1,2048]{1,0:T(1,128)S(1)}, f32[1,2048]{1,0:T(1,128)S(1)}, f32[1,2048]{1,0:T(1,128)S(1)}, f32[1,2048]{1,0:T(1,128)S(1)}) custom-call(bf16[2048,1024]{1,0:T(8,128)(2,1)S(1)} %multiply_convert_fusion.normed_ref, bf16[8192,1024]{1,0:T(8,128)(2,1)} %emb_ref.1, s32[1,2048]{1,0:T(1,128)S(1)} %bitcast.24), custom_call_target="tpu_custom_call" | custom-call | flops 34359738368 | bytes 21012480 | tf_op jit(solution)/shard_map/pallas_call | solution.py:75
  77.2 13.6 %all-gather.2 = f32[4,4,2048]{2,1,0:T(4,128)S(1)} all-gather(f32[1,4,2048]{2,1,0:T(4,128)S(1)} %maximum_bitcast_fusion), channel_id=3, replica_groups=mesh['req'=8,'tp'=4] {'tp'}, dimensions={0}, use_global_device_ids=true | all-gather | bytes 163840 | tf_op jit(solution)/shard_map/all_gather | solution.py:109
  90.8 0.1 fusion.7
  90.9 0.1 fusion.1
  91.0 1.3 %subtract_select_fusion = (f32[2048]{0:T(1024)}, f32[2048]{0:T(1024)}) fusion(f32[2048]{0:T(1024)S(1)} %get-tuple-element.12, f32[2048]{0:T(1024)S(1)} %get-tuple-element.13, f32[2048]{0:T(1024)S(1)} %get-tuple-element.18, s32[]{:T(128)} %dynamic-slice_reduce_fusion, f32[2048]{0:T(1024)S(1)} %get-tuple-element.17), kind=kLoop, calls=%fused_computation.14 | loop fusion | flops 14336 | bytes 49156 | tf_op jit(solution)/shard_map/jit(_where)/select_n | solution.py:119
  (3 shorter events, 0.0 us)
Async XLA Ops:
  0.6 18.6 %copy-start.1 = (f32[1024]{0:T(1024)S(1)}, f32[1024]{0:T(1024)}, u32[]{:S(2)}) copy-start(f32[1024]{0:T(1024)} %param.6) | copy-start | bytes 12292
  13.2 6.1 %copy-start = (f32[2048,1024]{1,0:T(8,128)S(1)}, f32[2048,1024]{1,0:T(8,128)}, u32[]{:S(2)}) copy-start(f32[2048,1024]{1,0:T(8,128)} %param.5) | copy-start | bytes 25165828

commit v6 on v5

--- a/solution.py
+++ b/solution.py
@@ -26,9 +26,15 @@
     return jnp.stack((peak, total, moment, chosen))
 
 
-def stats_kernel(row_block, normed_ref, emb_ref, ids_ref, peak_ref, total_ref, moment_ref, chosen_ref):
+LIFT = 40.0
+SAFE = 60.0
+
+
+def stats_kernel(row_block, normed_ref, emb_ref, ids_ref, peak_ref, total_ref, moment_ref, chosen_ref, saved_ref):
     j = pl.program_id(0)
     col_block = emb_ref.shape[0]
+    vocab_ids = lax.broadcasted_iota(jnp.int32, (col_block, row_block), 0)
+    stats = (peak_ref, total_ref, moment_ref, chosen_ref)
 
     @pl.when(j == 0)
     def _():
@@ -37,32 +43,69 @@
         moment_ref[...] = jnp.zeros(moment_ref.shape, jnp.float32)
         chosen_ref[...] = jnp.zeros(chosen_ref.shape, jnp.float32)
 
-    table = emb_ref[...]
-    vocab_ids = lax.broadcasted_iota(jnp.int32, (col_block, row_block), 0)
-
-    def chunk(r, carry):
-        start = pl.multiple_of(r * row_block, row_block)
-        rows = pl.ds(start, row_block)
-        logits = lax.dot_general(
-            table, normed_ref[rows, :], (((1,), (1,)), ((), ())),
+    def logits_of(rows):
+        return lax.dot_general(
+            emb_ref[...], normed_ref[rows, :], (((1,), (1,)), ((), ())),
             preferred_element_type=jnp.float32,
         )
+
+    def add_chosen(rows, logits):
+        local_id = ids_ref[:, rows] - j * col_block
+        chosen_ref[:, rows] = chosen_ref[:, rows] + jnp.sum(
+            jnp.where(vocab_ids == local_id, logits, 0.0), axis=0, keepdims=True
+        )
+
+    def rows_of(r):
+        return pl.ds(pl.multiple_of(r * row_block, row_block), row_block)
+
+    def exact_chunk(r, carry):
+        rows = rows_of(r)
+        logits = logits_of(rows)
         old_peak = peak_ref[:, rows]
         new_peak = jnp.maximum(old_peak, jnp.max(logits, axis=0, keepdims=True))
         weights = jnp.exp(logits - new_peak)
         scale = jnp.exp(old_peak - new_peak)
         total_ref[:, rows] = total_ref[:, rows] * scale + jnp.sum(weights, axis=0, keepdims=True)
-        moment_ref[:, rows] = moment_ref[:, rows] * scale + jnp.sum(
-            weights * logits, axis=0, keepdims=True
-        )
+        moment_ref[:, rows] = moment_ref[:, rows] * scale + jnp.sum(weights * logits, axis=0, keepdims=True)
         peak_ref[:, rows] = new_peak
-        local_id = ids_ref[:, rows] - j * col_block
-        chosen_ref[:, rows] = chosen_ref[:, rows] + jnp.sum(
-            jnp.where(vocab_ids == local_id, logits, 0.0), axis=0, keepdims=True
-        )
+        add_chosen(rows, logits)
         return carry
 
-    lax.fori_loop(0, normed_ref.shape[0] // row_block, chunk, 0, unroll=True)
+    def fast_chunk(r, worst):
+        rows = rows_of(r)
+        logits = logits_of(rows)
+        old_peak = peak_ref[:, rows]
+        shift = old_peak + LIFT
+        tile_peak = jnp.max(logits, axis=0, keepdims=True)
+        weights = jnp.exp(logits - shift)
+        new_peak = jnp.maximum(old_peak, tile_peak)
+        scale = jnp.exp(old_peak - new_peak)
+        part_scale = jnp.exp(shift - new_peak)
+        total_ref[:, rows] = total_ref[:, rows] * scale + jnp.sum(weights, axis=0, keepdims=True) * part_scale
+        moment_ref[:, rows] = moment_ref[:, rows] * scale + jnp.sum(weights * logits, axis=0, keepdims=True) * part_scale
+        peak_ref[:, rows] = new_peak
+        add_chosen(rows, logits)
+        return jnp.maximum(worst, tile_peak - old_peak)
+
+    n_chunks = normed_ref.shape[0] // row_block
+
+    @pl.when(j == 0)
+    def _():
+        lax.fori_loop(0, n_chunks, exact_chunk, 0, unroll=True)
+
+    @pl.when(j > 0)
+    def _():
+        for k, ref in enumerate(stats):
+            saved_ref[k:k + 1, :] = ref[...]
+        worst = lax.fori_loop(
+            0, n_chunks, fast_chunk, jnp.full((1, row_block), -1e30, jnp.float32), unroll=True
+        )
+
+        @pl.when(jnp.max(worst) > SAFE)
+        def _():
+            for k, ref in enumerate(stats):
+                ref[...] = saved_ref[k:k + 1, :]
+            lax.fori_loop(0, n_chunks, exact_chunk, 0, unroll=True)
 
 
 def shard_stats(normed, embedding, in_shard_id, col_block=1024, row_block=256):
@@ -82,6 +125,7 @@
         ],
         out_specs=[resident] * 4,
         out_shape=[stat] * 4,
+        scratch_shapes=[pltpu.VMEM((4, rows), jnp.float32)],
         compiler_params=pltpu.CompilerParams(
             dimension_semantics=("arbitrary",), vmem_limit_bytes=48 * 1024 * 1024
         ),

time: 92.6 us -> 87.1 us (0.941)
  Pallas kernels: 57 us -> 51.5 us
    pallas_call x1, Pallas kernels: 57 us -> 51.5 us  [shard_stats(): pl.pallas_call(functools.partial(stats_kernel, row_block), grid=(vocab //...]
where the time goes in v6:
time: 87.1 us; the launch traced here: 86.8 us
  Pallas kernels  51.5 us (59%)
  blocking collectives  23.1 us (27%)
  other arithmetic  9.33 us (11%)
  local copies, waits for them, and re-layouts  1.57 us (2%)
  between operations  1.36 us (2%)
    pallas_call x1, Pallas kernels, shard_stats(): pl.pallas_call(functools.partial(stats_kernel, row_block), grid=(vocab //...  51.5 us
    all_gather x1, blocking collectives, body(): gathered = lax.all_gather(stats, 'tp')  13.6 us
    unnamed x1, blocking collectives  9.47 us
    reduce_sum x1, other arithmetic, rms_normed(): mean_square = jnp.mean(states * states, axis=1, keepdims=True)  4.27 us

profile of v6, /device:TPU:0, one launch (start us, length us, event | category | flops | bytes accessed | tf_op | source)
XLA Modules:
  0.0 86.8 jit_solution(5205835646113922687)
XLA Ops:
  0.6 0.0 copy-start.1
  0.6 1.2 %dynamic-slice = u32[1]{0:T(128)} dynamic-slice(u32[32]{0:T(128)} %constant.41, u32[]{:T(128)S(6)} %add.23), dynamic_slice_sizes={1} | dynamic-slice | bytes 12
  2.5 0.7 add_select_fusion
  3.2 0.1 convert_reduce_fusion
  3.4 0.2 dynamic-update-slice
  3.6 0.1 reshape.33
  3.7 9.5 %all-reduce.1 = s32[8,8]{1,0:T(8,128)S(1)} all-reduce(s32[8,8]{1,0:T(8,128)S(1)} %reshape.33), channel_id=2, replica_groups=mesh['req'=8,'tp'=4] {'req'}, use_global_device_ids=true, to_apply=%add | all-reduce | flops 64 | bytes 512
  13.2 0.0 copy-start
  13.2 0.8 dynamic-slice_reduce_fusion
  13.9 1.0 %broadcast_subtract_fusion = s32[2048]{0:T(1024)S(1)} fusion(s32[2048]{0:T(1024)} %param.8, s32[]{:T(128)S(6)} %mul.33), kind=kLoop, calls=%fused_computation.24 | loop fusion | flops 2048 | bytes 16388 | tf_op jit(solution)/shard_map/sub | solution.py:152
  15.0 4.3 %multiply_reduce_fusion = f32[2048]{0:T(1024)S(1)} fusion(f32[2048,1024]{1,0:T(8,128)} %param.5), kind=kLoop, calls=%fused_computation.1 | loop fusion | flops 4192256 | bytes 8396800 | tf_op jit(solution)/shard_map/reduce_sum | solution.py:12
  19.2 0.0 copy-done.1
  19.3 0.0 copy-done
  19.3 0.9 %multiply_convert_fusion.normed_ref = bf16[2048,1024]{1,0:T(8,128)(2,1)S(1)} fusion(f32[2048,1024]{1,0:T(8,128)S(1)} %copy-done, f32[1024]{0:T(1024)S(1)} %copy-done.1, f32[2048]{0:T(1024)S(1)} %add_rsqrt_fusion), kind=kLoop, calls=%fused_computation | loop fusion | flops 6291456 | bytes 12595200 | tf_op jit(solution)/shard_map/convert_element_type | solution.py:13
  20.2 51.5 %shard_map.68 = (f32[1,2048]{1,0:T(1,128)S(1)}, f32[1,2048]{1,0:T(1,128)S(1)}, f32[1,2048]{1,0:T(1,128)S(1)}, f32[1,2048]{1,0:T(1,128)S(1)}) custom-call(bf16[2048,1024]{1,0:T(8,128)(2,1)S(1)} %multiply_convert_fusion.normed_ref, bf16[8192,1024]{1,0:T(8,128)(2,1)} %emb_ref.1, s32[1,2048]{1,0:T(1,128)S(1)} %bitcast.24), custom_call_target="tpu_custom_call" | custom-call | flops 34359738368 | bytes 21012480 | tf_op jit(solution)/shard_map/pallas_call | solution.py:118
  71.7 13.6 %all-gather.2 = f32[4,4,2048]{2,1,0:T(4,128)S(1)} all-gather(f32[1,4,2048]{2,1,0:T(4,128)S(1)} %maximum_bitcast_fusion), channel_id=3, replica_groups=mesh['req'=8,'tp'=4] {'tp'}, dimensions={0}, use_global_device_ids=true | all-gather | bytes 163840 | tf_op jit(solution)/shard_map/all_gather | solution.py:153
  85.3 0.1 fusion.7
  85.5 0.1 fusion.1
  85.5 1.3 %subtract_select_fusion = (f32[2048]{0:T(1024)}, f32[2048]{0:T(1024)}) fusion(f32[2048]{0:T(1024)S(1)} %get-tuple-element.12, f32[2048]{0:T(1024)S(1)} %get-tuple-element.13, f32[2048]{0:T(1024)S(1)} %get-tuple-element.18, s32[]{:T(128)} %dynamic-slice_reduce_fusion, f32[2048]{0:T(1024)S(1)} %get-tuple-element.17), kind=kLoop, calls=%fused_computation.14 | loop fusion | flops 14336 | bytes 49156 | tf_op jit(solution)/shard_map/jit(_where)/select_n | solution.py:163
  (3 shorter events, 0.0 us)
Async XLA Ops:
  0.6 18.6 %copy-start.1 = (f32[1024]{0:T(1024)S(1)}, f32[1024]{0:T(1024)}, u32[]{:S(2)}) copy-start(f32[1024]{0:T(1024)} %param.6) | copy-start | bytes 12292
  13.2 6.1 %copy-start = (f32[2048,1024]{1,0:T(8,128)S(1)}, f32[2048,1024]{1,0:T(8,128)}, u32[]{:S(2)}) copy-start(f32[2048,1024]{1,0:T(8,128)} %param.5) | copy-start | bytes 25165828

commit v7 on v6

--- a/solution.py
+++ b/solution.py
@@ -150,7 +150,13 @@
 
     normed = rms_normed(final_states, norm_gain)
     stats = shard_stats(normed, embedding, targets - vocab_start)
-    gathered = lax.all_gather(stats, "tp")
+    group = lax.axis_size("tp")
+    pieces = [stats]
+    for shift in range(1, group):
+        pieces.append(
+            lax.ppermute(stats, "tp", [(d, (d + shift) % group) for d in range(group)])
+        )
+    gathered = jnp.stack(pieces)
     peaks = gathered[:, 0]
     row_peak = jnp.max(peaks, axis=0)
     scale = jnp.exp(peaks - row_peak[None, :])

time: 87.1 us -> 80.4 us (0.923)
  blocking collectives: 23.1 us -> 8.02 us
  starting transfers between devices: 0 us -> 7.92 us
  other arithmetic: 9.33 us -> 10.4 us
    all_gather x1 -> x0, blocking collectives: 13.6 us -> none  [body(): gathered = lax.all_gather(stats, 'tp')]
    ppermute x0 -> x3, starting transfers between devices: none -> 7.92 us  [body(): lax.ppermute(stats, 'tp', [(d, (d + shift) % group) for d in range(group)])]
    convert_element_type x1, other arithmetic: 0.88 us -> 3.91 us  [rms_normed(): (states * lax.rsqrt(mean_square + 1e-06) * norm_gain[None, :]).astype(jnp...]
    unnamed x1, blocking collectives: 9.47 us -> 8.02 us
    sub x1, other arithmetic: 1.02 us -> 0.01 us  [body(): stats = shard_stats(normed, embedding, targets - vocab_start)]
  transfers between devices with their start and end apart: 0 -> 3, of which waited for: 0 -> 0; matrix products, arithmetic and copies ran while one was open for 0% -> 2% of each run, Pallas kernels for 0% -> 0%
where the time goes in v7:
time: 80.4 us; the launch traced here: 80.3 us
  Pallas kernels  51.5 us (64%)
  other arithmetic  10.4 us (13%)
  blocking collectives  8.02 us (10%)
  starting transfers between devices  7.92 us (10%)
  between operations  1.43 us (2%)
  local copies, waits for them, and re-layouts  0.93 us (1%)
    pallas_call x1, Pallas kernels, shard_stats(): pl.pallas_call(functools.partial(stats_kernel, row_block), grid=(vocab //...  51.5 us
    unnamed x1, blocking collectives  8.02 us
    ppermute x3, starting transfers between devices, body(): lax.ppermute(stats, 'tp', [(d, (d + shift) % group) for d in range(group)])  7.92 us
    reduce_sum x1, other arithmetic, rms_normed(): mean_square = jnp.mean(states * states, axis=1, keepdims=True)  4.01 us
    convert_element_type x1, other arithmetic, rms_normed(): (states * lax.rsqrt(mean_square + 1e-06) * norm_gain[None, :]).astype(jnp...  3.91 us
  transfers between devices with their start and end apart: 3, of which 0 were waited for; matrix products, arithmetic and copies ran while one was open for 2% of the time, Pallas kernels for 0%

profile of v7, /device:TPU:0, one launch (start us, length us, event | category | flops | bytes accessed | tf_op | source)
XLA Modules:
  0.0 80.3 jit_solution(5610323738103609855)
XLA Ops:
  0.6 0.0 copy-start
  0.6 0.0 copy-start.1
  0.7 4.0 %multiply_reduce_fusion = f32[2048]{0:T(1024)S(1)} fusion(f32[2048,1024]{1,0:T(8,128)} %param.5), kind=kLoop, calls=%fused_computation.1 | loop fusion | flops 4192256 | bytes 8396800 | tf_op jit(solution)/shard_map/reduce_sum | solution.py:12
  4.7 0.0 copy-done
  4.7 3.9 %multiply_convert_fusion.normed_ref = bf16[2048,1024]{1,0:T(8,128)(2,1)S(1)} fusion(f32[2048,1024]{1,0:T(8,128)} %param.5, f32[1024]{0:T(1024)S(1)} %copy-done.1, f32[2048]{0:T(1024)S(1)} %add_rsqrt_fusion), kind=kLoop, calls=%fused_computation | loop fusion | flops 6291456 | bytes 12595200 | tf_op jit(solution)/shard_map/convert_element_type | solution.py:13
  8.6 0.0 copy-start.2
  8.6 0.0 copy-start.3
  8.7 51.5 %shard_map.68 = (f32[1,2048]{1,0:T(1,128)S(1)}, f32[1,2048]{1,0:T(1,128)S(1)}, f32[1,2048]{1,0:T(1,128)S(1)}, f32[1,2048]{1,0:T(1,128)S(1)}) custom-call(bf16[2048,1024]{1,0:T(8,128)(2,1)S(1)} %multiply_convert_fusion.normed_ref, bf16[8192,1024]{1,0:T(8,128)(2,1)} %emb_ref.1, s32[1,2048]{1,0:T(1,128)S(1)} %bitcast.27), custom_call_target="tpu_custom_call" | custom-call | flops 34359738368 | bytes 21012480 | tf_op jit(solution)/shard_map/pallas_call | solution.py:118
  60.2 4.1 %collective-permute-start.1 = (f32[4,2048]{1,0:T(4,128)S(1)}, f32[4,2048]{1,0:T(4,128)S(1)}, u32[]{:S(2)}, u32[]{:S(2)}) collective-permute-start(f32[4,2048]{1,0:T(4,128)S(1)} %get-tuple-element.20), channel_id=1, source_target_pairs={{0,2},{1,3},{2,0},{3,1},{4,6},{5,7},{6,4},{7,5},{8,10},{9,11},{10,... | collective-permute-start | bytes 98312 | tf_op jit(solution)/shard_map/ppermute | solution.py:157
  64.3 1.6 %collective-permute-start = (f32[4,2048]{1,0:T(4,128)S(1)}, f32[4,2048]{1,0:T(4,128)S(1)}, u32[]{:S(2)}, u32[]{:S(2)}) collective-permute-start(f32[4,2048]{1,0:T(4,128)S(1)} %get-tuple-element.20), channel_id=1, source_target_pairs={{0,1},{1,2},{2,3},{3,0},{4,5},{5,6},{6,7},{7,4},{8,9},{9,10},{10,1... | collective-permute-start | bytes 98312 | tf_op jit(solution)/shard_map/ppermute | solution.py:157
  65.9 2.2 %collective-permute-start.2 = (f32[4,2048]{1,0:T(4,128)S(1)}, f32[4,2048]{1,0:T(4,128)S(1)}, u32[]{:S(2)}, u32[]{:S(2)}) collective-permute-start(f32[4,2048]{1,0:T(4,128)S(1)} %get-tuple-element.20), channel_id=1, source_target_pairs={{0,3},{1,0},{2,1},{3,2},{4,7},{5,4},{6,5},{7,6},{8,11},{9,8},{10,9... | collective-permute-start | bytes 98312 | tf_op jit(solution)/shard_map/ppermute | solution.py:157
  68.2 0.0 copy-done.2
  68.2 0.1 convert_reduce_fusion
  68.3 0.6 dynamic-slice
  69.6 0.2 dynamic-update-slice
  69.8 0.1 reshape.33
  69.9 8.0 %all-reduce.1 = s32[8,8]{1,0:T(8,128)S(1)} all-reduce(s32[8,8]{1,0:T(8,128)S(1)} %reshape.33), channel_id=2, replica_groups=mesh['req'=8,'tp'=4] {'req'}, use_global_device_ids=true, to_apply=%add | all-reduce | flops 64 | bytes 512
  77.9 0.8 dynamic-slice_reduce_fusion
  78.7 0.0 collective-permute-done.1
  78.7 0.0 collective-permute-done
  78.7 0.0 collective-permute-done.2
  78.7 0.1 fusion.8
  78.9 0.1 fusion.4
  79.0 1.3 %subtract_select_fusion = (f32[2048]{0:T(1024)}, f32[2048]{0:T(1024)}) fusion(f32[2048]{0:T(1024)S(1)} %get-tuple-element.12, f32[2048]{0:T(1024)S(1)} %get-tuple-element.13, f32[2048]{0:T(1024)S(1)} %get-tuple-element.18, s32[]{:T(128)} %dynamic-slice_reduce_fusion, f32[2048]{0:T(1024)S(1)} %get-tuple-element.17), kind=kLoop, calls=%fused_computation.15 | loop fusion | flops 14336 | bytes 49156 | tf_op jit(solution)/shard_map/jit(_where)/select_n | solution.py:169
  (8 shorter events, 0.1 us)
Async XLA Ops:
  0.6 4.1 %copy-start = (s32[2048]{0:T(1024)S(1)}, s32[2048]{0:T(1024)}, u32[]{:S(2)}) copy-start(s32[2048]{0:T(1024)} %param.8) | copy-start | bytes 24580
  0.6 4.1 %copy-start.1 = (f32[1024]{0:T(1024)S(1)}, f32[1024]{0:T(1024)}, u32[]{:S(2)}) copy-start(f32[1024]{0:T(1024)} %param.6) | copy-start | bytes 12292
  8.6 59.5 %copy-start.2 = (s32[1024]{0:T(1024)S(1)}, s32[1024]{0:T(1024)}, u32[]{:S(2)}) copy-start(s32[1024]{0:T(1024)} %param.9) | copy-start | bytes 12292
  8.6 59.7 %copy-start.3 = (u32[32]{0:T(128)S(1)}, u32[32]{0:T(128)}, u32[]{:S(2)}) copy-start(u32[32]{0:T(128)} %constant.41) | copy-start | bytes 388
  60.2 18.4 %collective-permute-start.1 = (f32[4,2048]{1,0:T(4,128)S(1)}, f32[4,2048]{1,0:T(4,128)S(1)}, u32[]{:S(2)}, u32[]{:S(2)}) collective-permute-start(f32[4,2048]{1,0:T(4,128)S(1)} %get-tuple-element.20), channel_id=1, source_target_pairs={{0,2},{1,3},{2,0},{3,1},{4,6},{5,7},{6,4},{7,5},{8,10},{9,11},{10,... | collective-permute-start | bytes 98312 | tf_op jit(solution)/shard_map/ppermute | solution.py:157
  64.3 14.4 %collective-permute-start = (f32[4,2048]{1,0:T(4,128)S(1)}, f32[4,2048]{1,0:T(4,128)S(1)}, u32[]{:S(2)}, u32[]{:S(2)}) collective-permute-start(f32[4,2048]{1,0:T(4,128)S(1)} %get-tuple-element.20), channel_id=1, source_target_pairs={{0,1},{1,2},{2,3},{3,0},{4,5},{5,6},{6,7},{7,4},{8,9},{9,10},{10,1... | collective-permute-start | bytes 98312 | tf_op jit(solution)/shard_map/ppermute | solution.py:157
  65.9 12.8 %collective-permute-start.2 = (f32[4,2048]{1,0:T(4,128)S(1)}, f32[4,2048]{1,0:T(4,128)S(1)}, u32[]{:S(2)}, u32[]{:S(2)}) collective-permute-start(f32[4,2048]{1,0:T(4,128)S(1)} %get-tuple-element.20), channel_id=1, source_target_pairs={{0,3},{1,0},{2,1},{3,2},{4,7},{5,4},{6,5},{7,6},{8,11},{9,8},{10,9... | collective-permute-start | bytes 98312 | tf_op jit(solution)/shard_map/ppermute | solution.py:157

commit v8 on v7

--- a/solution.py
+++ b/solution.py
@@ -30,7 +30,7 @@
 SAFE = 60.0
 
 
-def stats_kernel(row_block, normed_ref, emb_ref, ids_ref, peak_ref, total_ref, moment_ref, chosen_ref, saved_ref):
+def stats_kernel(row_block, states_ref, gain_ref, emb_ref, ids_ref, peak_ref, total_ref, moment_ref, chosen_ref, normed_ref, saved_ref):
     j = pl.program_id(0)
     col_block = emb_ref.shape[0]
     vocab_ids = lax.broadcasted_iota(jnp.int32, (col_block, row_block), 0)
@@ -38,6 +38,11 @@
 
     @pl.when(j == 0)
     def _():
+        for r in range(normed_ref.shape[0] // row_block):
+            rows = pl.ds(r * row_block, row_block)
+            x = states_ref[rows, :]
+            mean_square = jnp.mean(x * x, axis=1, keepdims=True)
+            normed_ref[rows, :] = (x * lax.rsqrt(mean_square + 1e-06) * gain_ref[...]).astype(jnp.bfloat16)
         peak_ref[...] = jnp.full(peak_ref.shape, -1e30, jnp.float32)
         total_ref[...] = jnp.zeros(total_ref.shape, jnp.float32)
         moment_ref[...] = jnp.zeros(moment_ref.shape, jnp.float32)
@@ -108,8 +113,8 @@
             lax.fori_loop(0, n_chunks, exact_chunk, 0, unroll=True)
 
 
-def shard_stats(normed, embedding, in_shard_id, col_block=1024, row_block=256):
-    rows, width = normed.shape
+def shard_stats(states, norm_gain, embedding, in_shard_id, col_block=1024, row_block=256):
+    rows, width = states.shape
     vocab = embedding.shape[0]
     col_block = min(col_block, vocab)
     row_block = min(row_block, rows)
@@ -120,21 +125,22 @@
         grid=(vocab // col_block,),
         in_specs=[
             pl.BlockSpec((rows, width), lambda j: (0, 0)),
+            pl.BlockSpec((1, width), lambda j: (0, 0)),
             pl.BlockSpec((col_block, width), lambda j: (j, 0)),
             pl.BlockSpec((1, rows), lambda j: (0, 0)),
         ],
         out_specs=[resident] * 4,
         out_shape=[stat] * 4,
-        scratch_shapes=[pltpu.VMEM((4, rows), jnp.float32)],
+        scratch_shapes=[pltpu.VMEM((rows, width), jnp.bfloat16), pltpu.VMEM((4, rows), jnp.float32)],
         compiler_params=pltpu.CompilerParams(
-            dimension_semantics=("arbitrary",), vmem_limit_bytes=48 * 1024 * 1024
+            dimension_semantics=("arbitrary",), vmem_limit_bytes=60 * 1024 * 1024
         ),
         cost_estimate=pl.CostEstimate(
             flops=2 * rows * vocab * width,
             transcendentals=rows * vocab,
-            bytes_accessed=rows * width * 2 + vocab * width * 2 + rows * 20,
+            bytes_accessed=rows * width * 4 + vocab * width * 2 + rows * 20,
         ),
-    )(normed, embedding, in_shard_id[None, :])
+    )(states, norm_gain[None, :], embedding, in_shard_id[None, :])
     return jnp.concatenate(outs, axis=0)
 
 
@@ -148,8 +154,7 @@
     live_count = jnp.sum(counts[:, lax.axis_index("req")])
     live = jnp.arange(own_rows, dtype=jnp.int32) < live_count
 
-    normed = rms_normed(final_states, norm_gain)
-    stats = shard_stats(normed, embedding, targets - vocab_start)
+    stats = shard_stats(final_states, norm_gain, embedding, targets - vocab_start)
     group = lax.axis_size("tp")
     pieces = [stats]
     for shift in range(1, group):

time: 80.4 us -> 78.2 us (0.973)
  other arithmetic: 10.4 us -> 4.54 us
  Pallas kernels: 51.5 us -> 55.2 us
    reduce_sum x1 -> x0, other arithmetic: 4.01 us -> none  [rms_normed(): mean_square = jnp.mean(states * states, axis=1, keepdims=True)]
    convert_element_type x1 -> x0, other arithmetic: 3.91 us -> none  [rms_normed(): (states * lax.rsqrt(mean_square + 1e-06) * norm_gain[None, :]).astype(jnp...]
    pallas_call x1, Pallas kernels: 51.5 us -> 55.2 us  [shard_stats(): pl.pallas_call(functools.partial(stats_kernel, row_block), grid=(vocab //...]
    sub x1, other arithmetic: 0.01 us -> 1.3 us  [body(): targets - vocab_start]
where the time goes in v8:
time: 78.2 us; the launch traced here: 78 us
  Pallas kernels  55.2 us (71%)
  blocking collectives  8.06 us (10%)
  starting transfers between devices  7.88 us (10%)
  other arithmetic  4.54 us (6%)
  between operations  1.34 us (2%)
  local copies, waits for them, and re-layouts  0.91 us (1%)
    pallas_call x1, Pallas kernels, shard_stats(): pl.pallas_call(functools.partial(stats_kernel, row_block), grid=(vocab //...  55.2 us
    unnamed x1, blocking collectives  8.06 us
    ppermute x3, starting transfers between devices, body(): lax.ppermute(stats, 'tp', [(d, (d + shift) % group) for d in range(group)])  7.88 us
  transfers between devices with their start and end apart: 3, of which 0 were waited for; matrix products, arithmetic and copies ran while one was open for 2% of the time, Pallas kernels for 0%

profile of v8, /device:TPU:0, one launch (start us, length us, event | category | flops | bytes accessed | tf_op | source)
XLA Modules:
  0.0 78.0 jit_solution(15165587180738297470)
XLA Ops:
  0.6 1.3 %broadcast_subtract_fusion = s32[2048]{0:T(1024)} fusion(s32[2048]{0:T(1024)} %param.8, s32[]{:T(128)S(6)} %mul.9), kind=kLoop, calls=%fused_computation.22 | loop fusion | flops 2048 | bytes 16388 | tf_op jit(solution)/shard_map/sub | solution.py:157
  1.9 0.0 copy-start
  1.9 0.0 copy-start.1
  1.9 55.2 %shard_map.68 = (f32[1,2048]{1,0:T(1,128)}, f32[1,2048]{1,0:T(1,128)}, f32[1,2048]{1,0:T(1,128)}, f32[1,2048]{1,0:T(1,128)}) custom-call(f32[2048,1024]{1,0:T(8,128)} %states_ref.1, f32[1,1024]{1,0:T(1,128)} %bitcast.32, bf16[8192,1024]{1,0:T(8,128)(2,1)} %emb_ref.1, s32[1,2048]{1,0:T(1,128)} %bitcast.31), custom_call_target="tpu_custom_call" | custom-call | flops 34359738368 | bytes 25206784 | tf_op jit(solution)/shard_map/pallas_call | solution.py:123
  57.1 0.8 %fusion.7 = (f32[1,4,2048]{2,1,0:T(4,128)S(1)}, f32[4,2048]{1,0:T(4,128)S(1)}) fusion(f32[1,2048]{1,0:T(1,128)} %get-tuple-element.9, f32[1,2048]{1,0:T(1,128)} %get-tuple-element.8, f32[1,2048]{1,0:T(1,128)} %get-tuple-element.7, f32[1,2048]{1,0:T(1,128)} %get-tuple-element.6), kind=kLoop, calls=%fused_computation.27 | loop fusion | flops 24576 | bytes 98304 | tf_op jit(solution)/shard_map/stack | solution.py:164
  57.9 4.1 %collective-permute-start.1 = (f32[4,2048]{1,0:T(4,128)S(1)}, f32[4,2048]{1,0:T(4,128)S(1)}, u32[]{:S(2)}, u32[]{:S(2)}) collective-permute-start(f32[4,2048]{1,0:T(4,128)S(1)} %get-tuple-element.20), channel_id=1, source_target_pairs={{0,2},{1,3},{2,0},{3,1},{4,6},{5,7},{6,4},{7,5},{8,10},{9,11},{10,... | collective-permute-start | bytes 98312 | tf_op jit(solution)/shard_map/ppermute | solution.py:162
  62.0 1.6 %collective-permute-start = (f32[4,2048]{1,0:T(4,128)S(1)}, f32[4,2048]{1,0:T(4,128)S(1)}, u32[]{:S(2)}, u32[]{:S(2)}) collective-permute-start(f32[4,2048]{1,0:T(4,128)S(1)} %get-tuple-element.20), channel_id=1, source_target_pairs={{0,1},{1,2},{2,3},{3,0},{4,5},{5,6},{6,7},{7,4},{8,9},{9,10},{10,1... | collective-permute-start | bytes 98312 | tf_op jit(solution)/shard_map/ppermute | solution.py:162
  63.6 2.2 %collective-permute-start.2 = (f32[4,2048]{1,0:T(4,128)S(1)}, f32[4,2048]{1,0:T(4,128)S(1)}, u32[]{:S(2)}, u32[]{:S(2)}) collective-permute-start(f32[4,2048]{1,0:T(4,128)S(1)} %get-tuple-element.20), channel_id=1, source_target_pairs={{0,3},{1,0},{2,1},{3,2},{4,7},{5,4},{6,5},{7,6},{8,11},{9,8},{10,9... | collective-permute-start | bytes 98312 | tf_op jit(solution)/shard_map/ppermute | solution.py:162
  65.8 0.0 copy-done
  65.8 0.1 convert_reduce_fusion
  65.9 0.0 copy-done.1
  66.0 0.6 dynamic-slice
  67.2 0.2 dynamic-update-slice
  67.4 0.1 reshape.24
  67.5 8.1 %all-reduce.1 = s32[8,8]{1,0:T(8,128)S(1)} all-reduce(s32[8,8]{1,0:T(8,128)S(1)} %reshape.24), channel_id=2, replica_groups=mesh['req'=8,'tp'=4] {'req'}, use_global_device_ids=true, to_apply=%add | all-reduce | flops 64 | bytes 512
  75.6 0.8 %dynamic-slice_reduce_fusion = s32[]{:T(128)} fusion(s32[8,8]{1,0:T(8,128)S(1)} %all-reduce.1, s32[]{:T(128)S(6)} %select_n.17), kind=kLoop, calls=%fused_computation.23 | loop fusion | flops 7 | bytes 40 | tf_op jit(solution)/shard_map/reduce_sum | solution.py:154
  76.4 0.0 collective-permute-done.1
  76.4 0.0 collective-permute-done
  76.4 0.0 collective-permute-done.2
  76.4 0.1 fusion.8
  76.6 0.1 fusion.4
  76.6 1.3 %subtract_select_fusion = (f32[2048]{0:T(1024)}, f32[2048]{0:T(1024)}) fusion(f32[2048]{0:T(1024)S(1)} %get-tuple-element.12, f32[2048]{0:T(1024)S(1)} %get-tuple-element.13, f32[2048]{0:T(1024)S(1)} %get-tuple-element.18, s32[]{:T(128)} %dynamic-slice_reduce_fusion, f32[2048]{0:T(1024)S(1)} %get-tuple-element.17), kind=kLoop, calls=%fused_computation.13 | loop fusion | flops 14336 | bytes 49156 | tf_op jit(solution)/shard_map/jit(_where)/select_n | solution.py:174
  (3 shorter events, 0.0 us)
Async XLA Ops:
  1.9 63.9 %copy-start = (s32[1024]{0:T(1024)S(1)}, s32[1024]{0:T(1024)}, u32[]{:S(2)}) copy-start(s32[1024]{0:T(1024)} %param.9) | copy-start | bytes 12292
  1.9 64.0 %copy-start.1 = (u32[32]{0:T(128)S(1)}, u32[32]{0:T(128)}, u32[]{:S(2)}) copy-start(u32[32]{0:T(128)} %constant.36) | copy-start | bytes 388
  57.9 18.4 %collective-permute-start.1 = (f32[4,2048]{1,0:T(4,128)S(1)}, f32[4,2048]{1,0:T(4,128)S(1)}, u32[]{:S(2)}, u32[]{:S(2)}) collective-permute-start(f32[4,2048]{1,0:T(4,128)S(1)} %get-tuple-element.20), channel_id=1, source_target_pairs={{0,2},{1,3},{2,0},{3,1},{4,6},{5,7},{6,4},{7,5},{8,10},{9,11},{10,... | collective-permute-start | bytes 98312 | tf_op jit(solution)/shard_map/ppermute | solution.py:162
  62.0 14.4 %collective-permute-start = (f32[4,2048]{1,0:T(4,128)S(1)}, f32[4,2048]{1,0:T(4,128)S(1)}, u32[]{:S(2)}, u32[]{:S(2)}) collective-permute-start(f32[4,2048]{1,0:T(4,128)S(1)} %get-tuple-element.20), channel_id=1, source_target_pairs={{0,1},{1,2},{2,3},{3,0},{4,5},{5,6},{6,7},{7,4},{8,9},{9,10},{10,1... | collective-permute-start | bytes 98312 | tf_op jit(solution)/shard_map/ppermute | solution.py:162
  63.6 12.8 %collective-permute-start.2 = (f32[4,2048]{1,0:T(4,128)S(1)}, f32[4,2048]{1,0:T(4,128)S(1)}, u32[]{:S(2)}, u32[]{:S(2)}) collective-permute-start(f32[4,2048]{1,0:T(4,128)S(1)} %get-tuple-element.20), channel_id=1, source_target_pairs={{0,3},{1,0},{2,1},{3,2},{4,7},{5,4},{6,5},{7,6},{8,11},{9,8},{10,9... | collective-permute-start | bytes 98312 | tf_op jit(solution)/shard_map/ppermute | solution.py:162

commit v9 on v8

--- a/solution.py
+++ b/solution.py
@@ -30,11 +30,11 @@
 SAFE = 60.0
 
 
-def stats_kernel(row_block, states_ref, gain_ref, emb_ref, ids_ref, peak_ref, total_ref, moment_ref, chosen_ref, normed_ref, saved_ref):
+def stats_kernel(row_block, states_ref, gain_ref, emb_ref, ids_ref, stats_ref, normed_ref, saved_ref):
     j = pl.program_id(0)
     col_block = emb_ref.shape[0]
     vocab_ids = lax.broadcasted_iota(jnp.int32, (col_block, row_block), 0)
-    stats = (peak_ref, total_ref, moment_ref, chosen_ref)
+    peak_ref, total_ref, moment_ref, chosen_ref = (stats_ref.at[k:k + 1] for k in range(4))
 
     @pl.when(j == 0)
     def _():
@@ -100,16 +100,14 @@
 
     @pl.when(j > 0)
     def _():
-        for k, ref in enumerate(stats):
-            saved_ref[k:k + 1, :] = ref[...]
+        saved_ref[...] = stats_ref[...]
         worst = lax.fori_loop(
             0, n_chunks, fast_chunk, jnp.full((1, row_block), -1e30, jnp.float32), unroll=True
         )
 
         @pl.when(jnp.max(worst) > SAFE)
         def _():
-            for k, ref in enumerate(stats):
-                ref[...] = saved_ref[k:k + 1, :]
+            stats_ref[...] = saved_ref[...]
             lax.fori_loop(0, n_chunks, exact_chunk, 0, unroll=True)
 
 
@@ -118,8 +116,8 @@
     vocab = embedding.shape[0]
     col_block = min(col_block, vocab)
     row_block = min(row_block, rows)
-    stat = jax.ShapeDtypeStruct((1, rows), jnp.float32)
-    resident = pl.BlockSpec((1, rows), lambda j: (0, 0))
+    stat = jax.ShapeDtypeStruct((4, rows), jnp.float32)
+    resident = pl.BlockSpec((4, rows), lambda j: (0, 0))
     outs = pl.pallas_call(
         functools.partial(stats_kernel, row_block),
         grid=(vocab // col_block,),
@@ -129,8 +127,8 @@
             pl.BlockSpec((col_block, width), lambda j: (j, 0)),
             pl.BlockSpec((1, rows), lambda j: (0, 0)),
         ],
-        out_specs=[resident] * 4,
-        out_shape=[stat] * 4,
+        out_specs=resident,
+        out_shape=stat,
         scratch_shapes=[pltpu.VMEM((rows, width), jnp.bfloat16), pltpu.VMEM((4, rows), jnp.float32)],
         compiler_params=pltpu.CompilerParams(
             dimension_semantics=("arbitrary",), vmem_limit_bytes=60 * 1024 * 1024
@@ -141,7 +139,7 @@
             bytes_accessed=rows * width * 4 + vocab * width * 2 + rows * 20,
         ),
     )(states, norm_gain[None, :], embedding, in_shard_id[None, :])
-    return jnp.concatenate(outs, axis=0)
+    return outs
 
 
 def body(final_states, norm_gain, embedding, targets, deal):
@@ -149,8 +147,8 @@
     own_rows = final_states.shape[0]
     shard_cols = embedding.shape[0]
     vocab_start = lax.axis_index("tp") * shard_cols
-    member = (deal[:, None] // own_rows == jnp.arange(owners, dtype=jnp.int32)[None, :])
-    counts = lax.all_gather(jnp.sum(member.astype(jnp.int32), axis=0), "req")
+    member = (jnp.arange(owners, dtype=jnp.int32)[:, None] == (deal // own_rows)[None, :])
+    counts = lax.all_gather(jnp.sum(member.astype(jnp.int32), axis=1), "req")
     live_count = jnp.sum(counts[:, lax.axis_index("req")])
     live = jnp.arange(own_rows, dtype=jnp.int32) < live_count
 

time: 78.2 us -> 76.1 us (0.973)
  starting transfers between devices: 7.88 us -> 6.07 us
    ppermute x3, starting transfers between devices: 7.88 us -> 6.07 us  [body(): lax.ppermute(stats, 'tp', [(d, (d + shift) % group) for d in range(group)])]
where the time goes in v9:
time: 76.1 us; the launch traced here: 75.8 us
  Pallas kernels  55.1 us (72%)
  blocking collectives  8.01 us (11%)
  starting transfers between devices  6.07 us (8%)
  other arithmetic  4.4 us (6%)
  between operations  1.33 us (2%)
  local copies, waits for them, and re-layouts  0.91 us (1%)
    pallas_call x1, Pallas kernels, shard_stats(): pl.pallas_call(functools.partial(stats_kernel, row_block), grid=(vocab //...  55.1 us
    unnamed x1, blocking collectives  8.01 us
    ppermute x3, starting transfers between devices, body(): lax.ppermute(stats, 'tp', [(d, (d + shift) % group) for d in range(group)])  6.07 us
  transfers between devices with their start and end apart: 3, of which 0 were waited for; matrix products, arithmetic and copies ran while one was open for 2% of the time, Pallas kernels for 0%

profile of v9, /device:TPU:0, one launch (start us, length us, event | category | flops | bytes accessed | tf_op | source)
XLA Modules:
  0.0 75.8 jit_solution(16481659985389283772)
XLA Ops:
  0.6 1.3 %broadcast_subtract_fusion = s32[2048]{0:T(1024)} fusion(s32[2048]{0:T(1024)} %param.8, s32[]{:T(128)S(6)} %mul.9), kind=kLoop, calls=%fused_computation.21 | loop fusion | flops 2048 | bytes 16388 | tf_op jit(solution)/shard_map/sub | solution.py:155
  1.9 0.0 copy-start
  1.9 0.0 copy-start.1
  1.9 55.1 %shard_map.68 = f32[4,2048]{1,0:T(4,128)} custom-call(f32[2048,1024]{1,0:T(8,128)} %states_ref.1, f32[1,1024]{1,0:T(1,128)} %bitcast.32, bf16[8192,1024]{1,0:T(8,128)(2,1)} %emb_ref.1, s32[1,2048]{1,0:T(1,128)} %bitcast.31), custom_call_target="tpu_custom_call" | custom-call | flops 34359738368 | bytes 25206784 | tf_op jit(solution)/shard_map/pallas_call | solution.py:121
  57.0 5.1 %collective-permute-start.2 = (f32[4,2048]{1,0:T(4,128)}, f32[4,2048]{1,0:T(4,128)S(1)}, u32[]{:S(2)}, u32[]{:S(2)}) collective-permute-start(f32[4,2048]{1,0:T(4,128)} %shard_map.68), channel_id=1, source_target_pairs={{0,3},{1,0},{2,1},{3,2},{4,7},{5,4},{6,5},{7,6},{8,11},{9,8},{10,9... | collective-permute-start | bytes 98312 | tf_op jit(solution)/shard_map/ppermute | solution.py:160
  62.1 0.0 collective-permute-start.1
  62.1 1.0 %collective-permute-start = (f32[4,2048]{1,0:T(4,128)}, f32[4,2048]{1,0:T(4,128)S(1)}, u32[]{:S(2)}, u32[]{:S(2)}) collective-permute-start(f32[4,2048]{1,0:T(4,128)} %shard_map.68), channel_id=1, source_target_pairs={{0,1},{1,2},{2,3},{3,0},{4,5},{5,6},{6,7},{7,4},{8,9},{9,10},{10,1... | collective-permute-start | bytes 98312 | tf_op jit(solution)/shard_map/ppermute | solution.py:160
  63.1 0.0 copy-done
  63.1 0.1 convert_reduce_fusion
  63.2 0.0 copy-done.1
  63.2 0.6 dynamic-slice
  64.5 0.2 dynamic-update-slice
  64.7 0.1 reshape.6
  64.8 8.0 %all-reduce.1 = s32[8,8]{1,0:T(8,128)S(1)} all-reduce(s32[8,8]{1,0:T(8,128)S(1)} %reshape.6), channel_id=2, replica_groups=mesh['req'=8,'tp'=4] {'req'}, use_global_device_ids=true, to_apply=%add | all-reduce | flops 64 | bytes 512
  72.8 0.7 dynamic-slice_reduce_fusion
  73.5 0.0 collective-permute-done.2
  73.5 0.0 collective-permute-done.1
  73.5 0.0 collective-permute-done
  73.6 0.8 %pad_maximum_fusion = f32[4,4,2048]{2,1,0:T(4,128)S(1)} fusion(f32[1,4,2048]{2,1,0:T(4,128)S(1)} %bitcast.28, f32[1,4,2048]{2,1,0:T(4,128)S(1)} %bitcast.29, f32[1,4,2048]{2,1,0:T(4,128)S(1)} %bitcast.30, f32[1,4,2048]{2,1,0:T(4,128)} %bitcast.27), kind=kLoop, calls=%fused_computation | loop fusion | flops 98304 | bytes 262144 | tf_op jit(solution)/shard_map/stack | solution.py:162
  74.3 0.1 fusion.7
  74.5 0.1 fusion.4
  74.6 1.2 %subtract_select_fusion = (f32[2048]{0:T(1024)}, f32[2048]{0:T(1024)}) fusion(f32[2048]{0:T(1024)S(1)} %get-tuple-element.4, f32[2048]{0:T(1024)S(1)} %get-tuple-element.5, f32[2048]{0:T(1024)S(1)} %get-tuple-element.10, s32[]{:T(128)} %dynamic-slice_reduce_fusion, f32[2048]{0:T(1024)S(1)} %get-tuple-element.9), kind=kLoop, calls=%fused_computation.12 | loop fusion | flops 14336 | bytes 49156 | tf_op jit(solution)/shard_map/jit(_where)/select_n | solution.py:172
  (2 shorter events, 0.0 us)
Async XLA Ops:
  1.9 61.2 %copy-start = (s32[1024]{0:T(1024)S(1)}, s32[1024]{0:T(1024)}, u32[]{:S(2)}) copy-start(s32[1024]{0:T(1024)} %param.9) | copy-start | bytes 12292
  1.9 61.3 %copy-start.1 = (u32[32]{0:T(128)S(1)}, u32[32]{0:T(128)}, u32[]{:S(2)}) copy-start(u32[32]{0:T(128)} %constant.36) | copy-start | bytes 388
  57.0 16.5 %collective-permute-start.2 = (f32[4,2048]{1,0:T(4,128)}, f32[4,2048]{1,0:T(4,128)S(1)}, u32[]{:S(2)}, u32[]{:S(2)}) collective-permute-start(f32[4,2048]{1,0:T(4,128)} %shard_map.68), channel_id=1, source_target_pairs={{0,3},{1,0},{2,1},{3,2},{4,7},{5,4},{6,5},{7,6},{8,11},{9,8},{10,9... | collective-permute-start | bytes 98312 | tf_op jit(solution)/shard_map/ppermute | solution.py:160
  62.1 11.5 %collective-permute-start.1 = (f32[4,2048]{1,0:T(4,128)}, f32[4,2048]{1,0:T(4,128)S(1)}, u32[]{:S(2)}, u32[]{:S(2)}) collective-permute-start(f32[4,2048]{1,0:T(4,128)} %shard_map.68), channel_id=1, source_target_pairs={{0,2},{1,3},{2,0},{3,1},{4,6},{5,7},{6,4},{7,5},{8,10},{9,11},{10,... | collective-permute-start | bytes 98312 | tf_op jit(solution)/shard_map/ppermute | solution.py:160
  62.1 11.5 %collective-permute-start = (f32[4,2048]{1,0:T(4,128)}, f32[4,2048]{1,0:T(4,128)S(1)}, u32[]{:S(2)}, u32[]{:S(2)}) collective-permute-start(f32[4,2048]{1,0:T(4,128)} %shard_map.68), channel_id=1, source_target_pairs={{0,1},{1,2},{2,3},{3,0},{4,5},{5,6},{6,7},{7,4},{8,9},{9,10},{10,1... | collective-permute-start | bytes 98312 | tf_op jit(solution)/shard_map/ppermute | solution.py:160

commit v10 on v9

--- a/solution.py
+++ b/solution.py
@@ -55,7 +55,7 @@
         )
 
     def add_chosen(rows, logits):
-        local_id = ids_ref[:, rows] - j * col_block
+        local_id = ids_ref[:, rows] - (lax.axis_index("tp") * pl.num_programs(0) + j) * col_block
         chosen_ref[:, rows] = chosen_ref[:, rows] + jnp.sum(
             jnp.where(vocab_ids == local_id, logits, 0.0), axis=0, keepdims=True
         )
@@ -146,13 +146,12 @@
     owners = lax.axis_size("req")
     own_rows = final_states.shape[0]
     shard_cols = embedding.shape[0]
-    vocab_start = lax.axis_index("tp") * shard_cols
     member = (jnp.arange(owners, dtype=jnp.int32)[:, None] == (deal // own_rows)[None, :])
     counts = lax.all_gather(jnp.sum(member.astype(jnp.int32), axis=1), "req")
     live_count = jnp.sum(counts[:, lax.axis_index("req")])
     live = jnp.arange(own_rows, dtype=jnp.int32) < live_count
 
-    stats = shard_stats(final_states, norm_gain, embedding, targets - vocab_start)
+    stats = shard_stats(final_states, norm_gain, embedding, targets)
     group = lax.axis_size("tp")
     pieces = [stats]
     for shift in range(1, group):

time: 76.1 us -> 75.6 us (level)
  other arithmetic: 4.4 us -> 3.11 us
  starting transfers between devices: 6.07 us -> 6.97 us
    sub x1 -> x0, other arithmetic: 1.3 us -> none  [body(): targets - vocab_start]
    ppermute x3, starting transfers between devices: 6.07 us -> 6.97 us  [body(): lax.ppermute(stats, 'tp', [(d, (d + shift) % group) for d in range(group)])]
where the time goes in v10:
time: 75.6 us; the launch traced here: 75.4 us
  Pallas kernels  55.1 us (73%)
  blocking collectives  8.01 us (11%)
  starting transfers between devices  6.97 us (9%)
  other arithmetic  3.11 us (4%)
  between operations  1.34 us (2%)
  local copies, waits for them, and re-layouts  0.92 us (1%)
    pallas_call x1, Pallas kernels, shard_stats(): pl.pallas_call(functools.partial(stats_kernel, row_block), grid=(vocab //...  55.1 us
    unnamed x1, blocking collectives  8.01 us
    ppermute x3, starting transfers between devices, body(): lax.ppermute(stats, 'tp', [(d, (d + shift) % group) for d in range(group)])  6.97 us
  transfers between devices with their start and end apart: 3, of which 0 were waited for; matrix products, arithmetic and copies ran while one was open for 2% of the time, Pallas kernels for 0%

profile of v10, /device:TPU:0, one launch (start us, length us, event | category | flops | bytes accessed | tf_op | source)
XLA Modules:
  0.0 75.4 jit_solution(18297724059231429311)
XLA Ops:
  0.6 0.0 copy-start
  0.6 0.0 copy-start.1
  0.7 55.1 %shard_map.68 = f32[4,2048]{1,0:T(4,128)} custom-call(f32[2048,1024]{1,0:T(8,128)} %states_ref.1, f32[1,1024]{1,0:T(1,128)} %bitcast.32, bf16[8192,1024]{1,0:T(8,128)(2,1)} %emb_ref.1, s32[1,2048]{1,0:T(1,128)} %bitcast.31), custom_call_target="tpu_custom_call" | custom-call | flops 34359738368 | bytes 25206784 | tf_op jit(solution)/shard_map/pallas_call | solution.py:121
  55.7 3.0 %collective-permute-start = (f32[4,2048]{1,0:T(4,128)}, f32[4,2048]{1,0:T(4,128)S(1)}, u32[]{:S(2)}, u32[]{:S(2)}) collective-permute-start(f32[4,2048]{1,0:T(4,128)} %shard_map.68), channel_id=1, source_target_pairs={{0,1},{1,2},{2,3},{3,0},{4,5},{5,6},{6,7},{7,4},{8,9},{9,10},{10,1... | collective-permute-start | bytes 98312 | tf_op jit(solution)/shard_map/ppermute | solution.py:159
  58.8 2.6 %collective-permute-start.1 = (f32[4,2048]{1,0:T(4,128)}, f32[4,2048]{1,0:T(4,128)S(1)}, u32[]{:S(2)}, u32[]{:S(2)}) collective-permute-start(f32[4,2048]{1,0:T(4,128)} %shard_map.68), channel_id=1, source_target_pairs={{0,2},{1,3},{2,0},{3,1},{4,6},{5,7},{6,4},{7,5},{8,10},{9,11},{10,... | collective-permute-start | bytes 98312 | tf_op jit(solution)/shard_map/ppermute | solution.py:159
  61.3 1.3 %collective-permute-start.2 = (f32[4,2048]{1,0:T(4,128)}, f32[4,2048]{1,0:T(4,128)S(1)}, u32[]{:S(2)}, u32[]{:S(2)}) collective-permute-start(f32[4,2048]{1,0:T(4,128)} %shard_map.68), channel_id=1, source_target_pairs={{0,3},{1,0},{2,1},{3,2},{4,7},{5,4},{6,5},{7,6},{8,11},{9,8},{10,9... | collective-permute-start | bytes 98312 | tf_op jit(solution)/shard_map/ppermute | solution.py:159
  62.7 0.0 copy-done
  62.7 0.1 convert_reduce_fusion
  62.8 0.0 copy-done.1
  62.8 0.6 dynamic-slice
  64.1 0.2 dynamic-update-slice
  64.3 0.1 reshape.6
  64.4 8.0 %all-reduce.1 = s32[8,8]{1,0:T(8,128)S(1)} all-reduce(s32[8,8]{1,0:T(8,128)S(1)} %reshape.6), channel_id=2, replica_groups=mesh['req'=8,'tp'=4] {'req'}, use_global_device_ids=true, to_apply=%add | all-reduce | flops 64 | bytes 512
  72.4 0.7 dynamic-slice_reduce_fusion
  73.1 0.0 collective-permute-done
  73.2 0.0 collective-permute-done.1
  73.2 0.0 collective-permute-done.2
  73.2 0.8 %pad_maximum_fusion = f32[4,4,2048]{2,1,0:T(4,128)S(1)} fusion(f32[1,4,2048]{2,1,0:T(4,128)S(1)} %bitcast.30, f32[1,4,2048]{2,1,0:T(4,128)S(1)} %bitcast.29, f32[1,4,2048]{2,1,0:T(4,128)S(1)} %bitcast.28, f32[1,4,2048]{2,1,0:T(4,128)} %bitcast.27), kind=kLoop, calls=%fused_computation | loop fusion | flops 98304 | bytes 262144 | tf_op jit(solution)/shard_map/stack | solution.py:161
  74.0 0.1 fusion.7
  74.1 0.1 fusion.4
  74.2 1.2 %subtract_select_fusion = (f32[2048]{0:T(1024)}, f32[2048]{0:T(1024)}) fusion(f32[2048]{0:T(1024)S(1)} %get-tuple-element.4, f32[2048]{0:T(1024)S(1)} %get-tuple-element.5, f32[2048]{0:T(1024)S(1)} %get-tuple-element.10, s32[]{:T(128)} %dynamic-slice_reduce_fusion, f32[2048]{0:T(1024)S(1)} %get-tuple-element.9), kind=kLoop, calls=%fused_computation.12 | loop fusion | flops 14336 | bytes 49156 | tf_op jit(solution)/shard_map/jit(_where)/select_n | solution.py:171
  (2 shorter events, 0.0 us)
Async XLA Ops:
  0.6 62.1 %copy-start = (s32[1024]{0:T(1024)S(1)}, s32[1024]{0:T(1024)}, u32[]{:S(2)}) copy-start(s32[1024]{0:T(1024)} %param.9) | copy-start | bytes 12292
  0.6 62.2 %copy-start.1 = (u32[32]{0:T(128)S(1)}, u32[32]{0:T(128)}, u32[]{:S(2)}) copy-start(u32[32]{0:T(128)} %constant.31) | copy-start | bytes 388
  55.7 17.4 %collective-permute-start = (f32[4,2048]{1,0:T(4,128)}, f32[4,2048]{1,0:T(4,128)S(1)}, u32[]{:S(2)}, u32[]{:S(2)}) collective-permute-start(f32[4,2048]{1,0:T(4,128)} %shard_map.68), channel_id=1, source_target_pairs={{0,1},{1,2},{2,3},{3,0},{4,5},{5,6},{6,7},{7,4},{8,9},{9,10},{10,1... | collective-permute-start | bytes 98312 | tf_op jit(solution)/shard_map/ppermute | solution.py:159
  58.8 14.4 %collective-permute-start.1 = (f32[4,2048]{1,0:T(4,128)}, f32[4,2048]{1,0:T(4,128)S(1)}, u32[]{:S(2)}, u32[]{:S(2)}) collective-permute-start(f32[4,2048]{1,0:T(4,128)} %shard_map.68), channel_id=1, source_target_pairs={{0,2},{1,3},{2,0},{3,1},{4,6},{5,7},{6,4},{7,5},{8,10},{9,11},{10,... | collective-permute-start | bytes 98312 | tf_op jit(solution)/shard_map/ppermute | solution.py:159
  61.3 11.8 %collective-permute-start.2 = (f32[4,2048]{1,0:T(4,128)}, f32[4,2048]{1,0:T(4,128)S(1)}, u32[]{:S(2)}, u32[]{:S(2)}) collective-permute-start(f32[4,2048]{1,0:T(4,128)} %shard_map.68), channel_id=1, source_target_pairs={{0,3},{1,0},{2,1},{3,2},{4,7},{5,4},{6,5},{7,6},{8,11},{9,8},{10,9... | collective-permute-start | bytes 98312 | tf_op jit(solution)/shard_map/ppermute | solution.py:159

commit v11 on v10

--- a/solution.py
+++ b/solution.py
@@ -147,8 +147,10 @@
     own_rows = final_states.shape[0]
     shard_cols = embedding.shape[0]
     member = (jnp.arange(owners, dtype=jnp.int32)[:, None] == (deal // own_rows)[None, :])
-    counts = lax.all_gather(jnp.sum(member.astype(jnp.int32), axis=1), "req")
-    live_count = jnp.sum(counts[:, lax.axis_index("req")])
+    local_counts = jnp.sum(member.astype(jnp.int32), axis=1)
+    first_copy = lax.axis_index("tp") == 0
+    counts = lax.psum(jnp.where(first_copy, local_counts, 0), ("req", "tp"))
+    live_count = counts[lax.axis_index("req")]
     live = jnp.arange(own_rows, dtype=jnp.int32) < live_count
 
     stats = shard_stats(final_states, norm_gain, embedding, targets)

time: 75.6 us -> 105 us (1.39)
  blocking collectives: 8.01 us -> 39.4 us
    psum x0 -> x1, blocking collectives: none -> 39.4 us  [body(): counts = lax.psum(jnp.where(first_copy, local_counts, 0), ('req', 'tp'))]
    unnamed x1 -> x0, blocking collectives: 8.01 us -> none
  transfers between devices with their start and end apart: 3 -> 3, of which waited for: 0 -> 0; matrix products, arithmetic and copies ran while one was open for 2% -> 1% of each run, Pallas kernels for 0% -> 0%
where the time goes in v11:
time: 105 us
  Pallas kernels  55.1 us (52%)
  blocking collectives  39.4 us (38%)
  starting transfers between devices  6.95 us (7%)
  other arithmetic  2.38 us (2%)
    pallas_call x1, Pallas kernels, shard_stats(): pl.pallas_call(functools.partial(stats_kernel, row_block), grid=(vocab //...  55.1 us
    psum x1, blocking collectives, body(): counts = lax.psum(jnp.where(first_copy, local_counts, 0), ('req', 'tp'))  39.4 us
    ppermute x3, starting transfers between devices, body(): lax.ppermute(stats, 'tp', [(d, (d + shift) % group) for d in range(group)])  6.95 us
  transfers between devices with their start and end apart: 3, of which 0 were waited for; matrix products, arithmetic and copies ran while one was open for 1% of the time, Pallas kernels for 0%

profile of v11, /device:TPU:0, one launch (start us, length us, event | category | flops | bytes accessed | tf_op | source)
XLA Modules:
  0.0 105.1 jit_solution(14627314759759878130)
XLA Ops:
  0.6 0.0 copy-start
  0.6 55.1 %shard_map.68 = f32[4,2048]{1,0:T(4,128)} custom-call(f32[2048,1024]{1,0:T(8,128)} %states_ref.1, f32[1,1024]{1,0:T(1,128)} %bitcast.32, bf16[8192,1024]{1,0:T(8,128)(2,1)} %emb_ref.1, s32[1,2048]{1,0:T(1,128)} %bitcast.31), custom_call_target="tpu_custom_call" | custom-call | flops 34359738368 | bytes 25206784 | tf_op jit(solution)/shard_map/pallas_call | solution.py:121
  55.7 3.0 %collective-permute-start = (f32[4,2048]{1,0:T(4,128)}, f32[4,2048]{1,0:T(4,128)S(1)}, u32[]{:S(2)}, u32[]{:S(2)}) collective-permute-start(f32[4,2048]{1,0:T(4,128)} %shard_map.68), channel_id=1, source_target_pairs={{0,1},{1,2},{2,3},{3,0},{4,5},{5,6},{6,7},{7,4},{8,9},{9,10},{10,1... | collective-permute-start | bytes 98312 | tf_op jit(solution)/shard_map/ppermute | solution.py:161
  58.7 2.6 %collective-permute-start.1 = (f32[4,2048]{1,0:T(4,128)}, f32[4,2048]{1,0:T(4,128)S(1)}, u32[]{:S(2)}, u32[]{:S(2)}) collective-permute-start(f32[4,2048]{1,0:T(4,128)} %shard_map.68), channel_id=1, source_target_pairs={{0,2},{1,3},{2,0},{3,1},{4,6},{5,7},{6,4},{7,5},{8,10},{9,11},{10,... | collective-permute-start | bytes 98312 | tf_op jit(solution)/shard_map/ppermute | solution.py:161
  61.3 1.3 %collective-permute-start.2 = (f32[4,2048]{1,0:T(4,128)}, f32[4,2048]{1,0:T(4,128)S(1)}, u32[]{:S(2)}, u32[]{:S(2)}) collective-permute-start(f32[4,2048]{1,0:T(4,128)} %shard_map.68), channel_id=1, source_target_pairs={{0,3},{1,0},{2,1},{3,2},{4,7},{5,4},{6,5},{7,6},{8,11},{9,8},{10,9... | collective-permute-start | bytes 98312 | tf_op jit(solution)/shard_map/ppermute | solution.py:161
  62.7 0.0 copy-done
  62.7 0.1 convert_reduce_fusion
  62.8 39.4 %psum.7 = s32[8]{0:T(128)S(1)} all-reduce(s32[8]{0:T(128)S(1)} %broadcast_select_fusion), channel_id=1, replica_groups=mesh['req'=8,'tp'=4] {'req','tp'}, use_global_device_ids=true, to_apply=%region_1.2 | all-reduce | flops 8 | bytes 64 | tf_op jit(solution)/shard_map/psum | solution.py:152
  102.2 0.6 dynamic_slice.3
  102.8 0.0 collective-permute-done
  102.8 0.0 collective-permute-done.1
  102.9 0.0 collective-permute-done.2
  102.9 0.8 pad_maximum_fusion
  103.7 0.1 fusion.7
  103.8 0.1 fusion.4
  103.9 1.2 %subtract_select_fusion = (f32[2048]{0:T(1024)}, f32[2048]{0:T(1024)}) fusion(f32[2048]{0:T(1024)S(1)} %get-tuple-element.4, f32[2048]{0:T(1024)S(1)} %get-tuple-element.5, f32[2048]{0:T(1024)S(1)} %get-tuple-element.10, s32[]{:T(128)} %bitcast, f32[2048]{0:T(1024)S(1)} %get-tuple-element.9), kind=kLoop, calls=%fused_computation.12 | loop fusion | flops 14336 | bytes 49156 | tf_op jit(solution)/shard_map/jit(_where)/select_n | solution.py:173
  (2 shorter events, 0.0 us)
Async XLA Ops:
  0.6 62.0 %copy-start = (s32[1024]{0:T(1024)S(1)}, s32[1024]{0:T(1024)}, u32[]{:S(2)}) copy-start(s32[1024]{0:T(1024)} %param.9) | copy-start | bytes 12292
  55.7 47.1 %collective-permute-start = (f32[4,2048]{1,0:T(4,128)}, f32[4,2048]{1,0:T(4,128)S(1)}, u32[]{:S(2)}, u32[]{:S(2)}) collective-permute-start(f32[4,2048]{1,0:T(4,128)} %shard_map.68), channel_id=1, source_target_pairs={{0,1},{1,2},{2,3},{3,0},{4,5},{5,6},{6,7},{7,4},{8,9},{9,10},{10,1... | collective-permute-start | bytes 98312 | tf_op jit(solution)/shard_map/ppermute | solution.py:161
  58.7 44.1 %collective-permute-start.1 = (f32[4,2048]{1,0:T(4,128)}, f32[4,2048]{1,0:T(4,128)S(1)}, u32[]{:S(2)}, u32[]{:S(2)}) collective-permute-start(f32[4,2048]{1,0:T(4,128)} %shard_map.68), channel_id=1, source_target_pairs={{0,2},{1,3},{2,0},{3,1},{4,6},{5,7},{6,4},{7,5},{8,10},{9,11},{10,... | collective-permute-start | bytes 98312 | tf_op jit(solution)/shard_map/ppermute | solution.py:161
  61.3 41.5 %collective-permute-start.2 = (f32[4,2048]{1,0:T(4,128)}, f32[4,2048]{1,0:T(4,128)S(1)}, u32[]{:S(2)}, u32[]{:S(2)}) collective-permute-start(f32[4,2048]{1,0:T(4,128)} %shard_map.68), channel_id=1, source_target_pairs={{0,3},{1,0},{2,1},{3,2},{4,7},{5,4},{6,5},{7,6},{8,11},{9,8},{10,9... | collective-permute-start | bytes 98312 | tf_op jit(solution)/shard_map/ppermute | solution.py:161

commit v12 on v10

--- a/solution.py
+++ b/solution.py
@@ -30,7 +30,7 @@
 SAFE = 60.0
 
 
-def stats_kernel(row_block, states_ref, gain_ref, emb_ref, ids_ref, stats_ref, normed_ref, saved_ref):
+def stats_kernel(row_block, states_ref, gain_ref, emb_ref, ids_ref, stats_ref, normed_ref, saved_ref, states_vmem, copy_sems):
     j = pl.program_id(0)
     col_block = emb_ref.shape[0]
     vocab_ids = lax.broadcasted_iota(jnp.int32, (col_block, row_block), 0)
@@ -38,9 +38,20 @@
 
     @pl.when(j == 0)
     def _():
-        for r in range(normed_ref.shape[0] // row_block):
+        copies = [
+            pltpu.make_async_copy(
+                states_ref.at[pl.ds(r * row_block, row_block)],
+                states_vmem.at[pl.ds(r * row_block, row_block)],
+                copy_sems.at[r],
+            )
+            for r in range(normed_ref.shape[0] // row_block)
+        ]
+        for copy in copies:
+            copy.start()
+        for r, copy in enumerate(copies):
             rows = pl.ds(r * row_block, row_block)
-            x = states_ref[rows, :]
+            copy.wait()
+            x = states_vmem[rows, :]
             mean_square = jnp.mean(x * x, axis=1, keepdims=True)
             normed_ref[rows, :] = (x * lax.rsqrt(mean_square + 1e-06) * gain_ref[...]).astype(jnp.bfloat16)
         peak_ref[...] = jnp.full(peak_ref.shape, -1e30, jnp.float32)
@@ -122,14 +133,19 @@
         functools.partial(stats_kernel, row_block),
         grid=(vocab // col_block,),
         in_specs=[
-            pl.BlockSpec((rows, width), lambda j: (0, 0)),
+            pl.BlockSpec(memory_space=pl.ANY),
             pl.BlockSpec((1, width), lambda j: (0, 0)),
             pl.BlockSpec((col_block, width), lambda j: (j, 0)),
             pl.BlockSpec((1, rows), lambda j: (0, 0)),
         ],
         out_specs=resident,
         out_shape=stat,
-        scratch_shapes=[pltpu.VMEM((rows, width), jnp.bfloat16), pltpu.VMEM((4, rows), jnp.float32)],
+        scratch_shapes=[
+            pltpu.VMEM((rows, width), jnp.bfloat16),
+            pltpu.VMEM((4, rows), jnp.float32),
+            pltpu.VMEM((rows, width), jnp.float32),
+            pltpu.SemaphoreType.DMA((rows // row_block,)),
+        ],
         compiler_params=pltpu.CompilerParams(
             dimension_semantics=("arbitrary",), vmem_limit_bytes=60 * 1024 * 1024
         ),

time: 75.6 us -> 76.2 us (level)
  no operation moved by 1% of the time
where the time goes in v12:
time: 76.2 us; the launch traced here: 76 us
  Pallas kernels  55.6 us (73%)
  blocking collectives  8.02 us (11%)
  starting transfers between devices  7.01 us (9%)
  other arithmetic  3.11 us (4%)
  between operations  1.35 us (2%)
  local copies, waits for them, and re-layouts  0.92 us (1%)
    pallas_call x1, Pallas kernels, shard_stats(): pl.pallas_call(functools.partial(stats_kernel, row_block), grid=(vocab //...  55.6 us
    unnamed x1, blocking collectives  8.02 us
    ppermute x3, starting transfers between devices, body(): lax.ppermute(stats, 'tp', [(d, (d + shift) % group) for d in range(group)])  7.01 us
  transfers between devices with their start and end apart: 3, of which 0 were waited for; matrix products, arithmetic and copies ran while one was open for 2% of the time, Pallas kernels for 0%

profile of v12, /device:TPU:0, one launch (start us, length us, event | category | flops | bytes accessed | tf_op | source)
XLA Modules:
  0.0 76.0 jit_solution(16599221684301339965)
XLA Ops:
  0.6 0.0 copy-start
  0.6 0.0 copy-start.1
  0.7 55.6 %shard_map.68 = f32[4,2048]{1,0:T(4,128)} custom-call(f32[2048,1024]{1,0:T(8,128)} %states_ref.1, f32[1,1024]{1,0:T(1,128)} %bitcast.32, bf16[8192,1024]{1,0:T(8,128)(2,1)} %emb_ref.1, s32[1,2048]{1,0:T(1,128)} %bitcast.31), custom_call_target="tpu_custom_call" | custom-call | flops 34359738368 | bytes 25206784 | tf_op jit(solution)/shard_map/pallas_call | solution.py:132
  56.2 3.1 %collective-permute-start = (f32[4,2048]{1,0:T(4,128)}, f32[4,2048]{1,0:T(4,128)S(1)}, u32[]{:S(2)}, u32[]{:S(2)}) collective-permute-start(f32[4,2048]{1,0:T(4,128)} %shard_map.68), channel_id=1, source_target_pairs={{0,1},{1,2},{2,3},{3,0},{4,5},{5,6},{6,7},{7,4},{8,9},{9,10},{10,1... | collective-permute-start | bytes 98312 | tf_op jit(solution)/shard_map/ppermute | solution.py:175
  59.3 2.6 %collective-permute-start.1 = (f32[4,2048]{1,0:T(4,128)}, f32[4,2048]{1,0:T(4,128)S(1)}, u32[]{:S(2)}, u32[]{:S(2)}) collective-permute-start(f32[4,2048]{1,0:T(4,128)} %shard_map.68), channel_id=1, source_target_pairs={{0,2},{1,3},{2,0},{3,1},{4,6},{5,7},{6,4},{7,5},{8,10},{9,11},{10,... | collective-permute-start | bytes 98312 | tf_op jit(solution)/shard_map/ppermute | solution.py:175
  61.9 1.3 %collective-permute-start.2 = (f32[4,2048]{1,0:T(4,128)}, f32[4,2048]{1,0:T(4,128)S(1)}, u32[]{:S(2)}, u32[]{:S(2)}) collective-permute-start(f32[4,2048]{1,0:T(4,128)} %shard_map.68), channel_id=1, source_target_pairs={{0,3},{1,0},{2,1},{3,2},{4,7},{5,4},{6,5},{7,6},{8,11},{9,8},{10,9... | collective-permute-start | bytes 98312 | tf_op jit(solution)/shard_map/ppermute | solution.py:175
  63.3 0.0 copy-done
  63.3 0.1 convert_reduce_fusion
  63.4 0.0 copy-done.1
  63.4 0.6 dynamic-slice
  64.7 0.2 dynamic-update-slice
  64.9 0.1 reshape.6
  65.0 8.0 %all-reduce.1 = s32[8,8]{1,0:T(8,128)S(1)} all-reduce(s32[8,8]{1,0:T(8,128)S(1)} %reshape.6), channel_id=2, replica_groups=mesh['req'=8,'tp'=4] {'req'}, use_global_device_ids=true, to_apply=%add | all-reduce | flops 64 | bytes 512
  73.0 0.7 dynamic-slice_reduce_fusion
  73.7 0.0 collective-permute-done
  73.7 0.0 collective-permute-done.1
  73.7 0.0 collective-permute-done.2
  73.7 0.8 %pad_maximum_fusion = f32[4,4,2048]{2,1,0:T(4,128)S(1)} fusion(f32[1,4,2048]{2,1,0:T(4,128)S(1)} %bitcast.30, f32[1,4,2048]{2,1,0:T(4,128)S(1)} %bitcast.29, f32[1,4,2048]{2,1,0:T(4,128)S(1)} %bitcast.28, f32[1,4,2048]{2,1,0:T(4,128)} %bitcast.27), kind=kLoop, calls=%fused_computation | loop fusion | flops 98304 | bytes 262144 | tf_op jit(solution)/shard_map/stack | solution.py:177
  74.5 0.1 fusion.7
  74.7 0.1 fusion.4
  74.8 1.2 %subtract_select_fusion = (f32[2048]{0:T(1024)}, f32[2048]{0:T(1024)}) fusion(f32[2048]{0:T(1024)S(1)} %get-tuple-element.4, f32[2048]{0:T(1024)S(1)} %get-tuple-element.5, f32[2048]{0:T(1024)S(1)} %get-tuple-element.10, s32[]{:T(128)} %dynamic-slice_reduce_fusion, f32[2048]{0:T(1024)S(1)} %get-tuple-element.9), kind=kLoop, calls=%fused_computation.12 | loop fusion | flops 14336 | bytes 49156 | tf_op jit(solution)/shard_map/jit(_where)/select_n | solution.py:187
  (2 shorter events, 0.0 us)
Async XLA Ops:
  0.6 62.6 %copy-start = (s32[1024]{0:T(1024)S(1)}, s32[1024]{0:T(1024)}, u32[]{:S(2)}) copy-start(s32[1024]{0:T(1024)} %param.9) | copy-start | bytes 12292
  0.6 62.8 %copy-start.1 = (u32[32]{0:T(128)S(1)}, u32[32]{0:T(128)}, u32[]{:S(2)}) copy-start(u32[32]{0:T(128)} %constant.31) | copy-start | bytes 388
  56.2 17.5 %collective-permute-start = (f32[4,2048]{1,0:T(4,128)}, f32[4,2048]{1,0:T(4,128)S(1)}, u32[]{:S(2)}, u32[]{:S(2)}) collective-permute-start(f32[4,2048]{1,0:T(4,128)} %shard_map.68), channel_id=1, source_target_pairs={{0,1},{1,2},{2,3},{3,0},{4,5},{5,6},{6,7},{7,4},{8,9},{9,10},{10,1... | collective-permute-start | bytes 98312 | tf_op jit(solution)/shard_map/ppermute | solution.py:175
  59.3 14.4 %collective-permute-start.1 = (f32[4,2048]{1,0:T(4,128)}, f32[4,2048]{1,0:T(4,128)S(1)}, u32[]{:S(2)}, u32[]{:S(2)}) collective-permute-start(f32[4,2048]{1,0:T(4,128)} %shard_map.68), channel_id=1, source_target_pairs={{0,2},{1,3},{2,0},{3,1},{4,6},{5,7},{6,4},{7,5},{8,10},{9,11},{10,... | collective-permute-start | bytes 98312 | tf_op jit(solution)/shard_map/ppermute | solution.py:175
  61.9 11.8 %collective-permute-start.2 = (f32[4,2048]{1,0:T(4,128)}, f32[4,2048]{1,0:T(4,128)S(1)}, u32[]{:S(2)}, u32[]{:S(2)}) collective-permute-start(f32[4,2048]{1,0:T(4,128)} %shard_map.68), channel_id=1, source_target_pairs={{0,3},{1,0},{2,1},{3,2},{4,7},{5,4},{6,5},{7,6},{8,11},{9,8},{10,9... | collective-permute-start | bytes 98312 | tf_op jit(solution)/shard_map/ppermute | solution.py:175

commit v13 on v10

--- a/solution.py
+++ b/solution.py
@@ -158,13 +158,11 @@
         pieces.append(
             lax.ppermute(stats, "tp", [(d, (d + shift) % group) for d in range(group)])
         )
-    gathered = jnp.stack(pieces)
-    peaks = gathered[:, 0]
-    row_peak = jnp.max(peaks, axis=0)
-    scale = jnp.exp(peaks - row_peak[None, :])
-    exp_total = jnp.sum(gathered[:, 1] * scale, axis=0)
-    moment = jnp.sum(gathered[:, 2] * scale, axis=0)
-    chosen = jnp.sum(gathered[:, 3], axis=0)
+    row_peak = functools.reduce(jnp.maximum, [piece[0] for piece in pieces])
+    scales = [jnp.exp(piece[0] - row_peak) for piece in pieces]
+    exp_total = sum(piece[1] * s for piece, s in zip(pieces, scales))
+    moment = sum(piece[2] * s for piece, s in zip(pieces, scales))
+    chosen = sum(piece[3] for piece in pieces)
     log_total = row_peak + jnp.log(exp_total)
     expected = moment / exp_total
     logprob = jnp.where(live, chosen - log_total, 0.0)

time: 75.6 us -> 75.7 us (level)
    slice x1, other arithmetic: 0.14 us -> 1 us  [body(): moment = sum((piece[2] * s for piece, s in zip(pieces, scales)))]
    another operation x1 -> x0, other arithmetic: 0.79 us -> none  [body(): gathered = jnp.stack(pieces)]
where the time goes in v13:
time: 75.7 us; the launch traced here: 75.4 us
  Pallas kernels  55.1 us (73%)
  blocking collectives  8.01 us (11%)
  starting transfers between devices  6.97 us (9%)
  other arithmetic  3.13 us (4%)
  between operations  1.33 us (2%)
  local copies, waits for them, and re-layouts  0.92 us (1%)
    pallas_call x1, Pallas kernels, shard_stats(): pl.pallas_call(functools.partial(stats_kernel, row_block), grid=(vocab //...  55.1 us
    unnamed x1, blocking collectives  8.01 us
    ppermute x3, starting transfers between devices, body(): lax.ppermute(stats, 'tp', [(d, (d + shift) % group) for d in range(group)])  6.97 us
  transfers between devices with their start and end apart: 3, of which 0 were waited for; matrix products, arithmetic and copies ran while one was open for 2% of the time, Pallas kernels for 0%

profile of v13, /device:TPU:0, one launch (start us, length us, event | category | flops | bytes accessed | tf_op | source)
XLA Modules:
  0.0 75.4 jit_solution(11685776976754451709)
XLA Ops:
  0.6 0.0 copy-start
  0.6 0.0 copy-start.1
  0.7 55.1 %shard_map.68 = f32[4,2048]{1,0:T(4,128)} custom-call(f32[2048,1024]{1,0:T(8,128)} %states_ref.1, f32[1,1024]{1,0:T(1,128)} %bitcast.30, bf16[8192,1024]{1,0:T(8,128)(2,1)} %emb_ref.1, s32[1,2048]{1,0:T(1,128)} %bitcast.29), custom_call_target="tpu_custom_call" | custom-call | flops 34359738368 | bytes 25206784 | tf_op jit(solution)/shard_map/pallas_call | solution.py:121
  55.7 3.0 %collective-permute-start = (f32[4,2048]{1,0:T(4,128)}, f32[4,2048]{1,0:T(4,128)S(1)}, u32[]{:S(2)}, u32[]{:S(2)}) collective-permute-start(f32[4,2048]{1,0:T(4,128)} %shard_map.68), channel_id=1, source_target_pairs={{0,1},{1,2},{2,3},{3,0},{4,5},{5,6},{6,7},{7,4},{8,9},{9,10},{10,1... | collective-permute-start | bytes 98312 | tf_op jit(solution)/shard_map/ppermute | solution.py:159
  58.8 2.6 %collective-permute-start.1 = (f32[4,2048]{1,0:T(4,128)}, f32[4,2048]{1,0:T(4,128)S(1)}, u32[]{:S(2)}, u32[]{:S(2)}) collective-permute-start(f32[4,2048]{1,0:T(4,128)} %shard_map.68), channel_id=1, source_target_pairs={{0,2},{1,3},{2,0},{3,1},{4,6},{5,7},{6,4},{7,5},{8,10},{9,11},{10,... | collective-permute-start | bytes 98312 | tf_op jit(solution)/shard_map/ppermute | solution.py:159
  61.3 1.3 %collective-permute-start.2 = (f32[4,2048]{1,0:T(4,128)}, f32[4,2048]{1,0:T(4,128)S(1)}, u32[]{:S(2)}, u32[]{:S(2)}) collective-permute-start(f32[4,2048]{1,0:T(4,128)} %shard_map.68), channel_id=1, source_target_pairs={{0,3},{1,0},{2,1},{3,2},{4,7},{5,4},{6,5},{7,6},{8,11},{9,8},{10,9... | collective-permute-start | bytes 98312 | tf_op jit(solution)/shard_map/ppermute | solution.py:159
  62.7 0.0 copy-done
  62.7 0.1 convert_reduce_fusion
  62.8 0.0 copy-done.1
  62.8 0.6 dynamic-slice
  64.1 0.2 dynamic-update-slice
  64.3 0.1 reshape.8
  64.4 8.0 %all-reduce.1 = s32[8,8]{1,0:T(8,128)S(1)} all-reduce(s32[8,8]{1,0:T(8,128)S(1)} %reshape.8), channel_id=2, replica_groups=mesh['req'=8,'tp'=4] {'req'}, use_global_device_ids=true, to_apply=%add | all-reduce | flops 64 | bytes 512
  72.4 0.7 dynamic-slice_reduce_fusion
  73.1 0.0 collective-permute-done
  73.2 0.0 collective-permute-done.1
  73.2 0.0 collective-permute-done.2
  73.2 1.0 %fusion.2 = (f32[1,2048]{1,0:T(1,128)S(1)}, f32[1,2048]{1,0:T(1,128)S(1)}, f32[1,2048]{1,0:T(1,128)S(1)}, f32[1,2048]{1,0:T(1,128)S(1)}, f32[1,2048]{1,0:T(1,128...) fusion(f32[4,2048]{1,0:T(4,128)} %shard_map.68, ...), kind=kLoop, calls=%fused_computation.23 | loop fusion | flops 6144 | bytes 237568 | tf_op jit(solution)/shard_map/slice | solution.py:164
  74.2 1.3 %subtract_select_fusion = (f32[2048]{0:T(1024)}, f32[2048]{0:T(1024)}) fusion(f32[2048]{0:T(1024)S(1)} %bitcast.22, f32[2048]{0:T(1024)S(1)} %bitcast.21, f32[2048]{0:T(1024)S(1)} %bitcast.20, f32[2048]{0:T(1024)S(1)} %bitcast.16, s32[]{:T(128)} %dynamic-slice_reduce_fusion, f32[2048]{0:T(1024)S(1)} %bitcast.18, f32[2048]{0:T(1024)S(1)} %bitcast.28, ...), kind=kLoop, calls=%fused_computation.5 | loop fusion | flops 57344 | bytes 122884 | tf_op jit(solution)/shard_map/jit(_where)/select_n | solution.py:169
  (2 shorter events, 0.0 us)
Async XLA Ops:
  0.6 62.1 %copy-start = (s32[1024]{0:T(1024)S(1)}, s32[1024]{0:T(1024)}, u32[]{:S(2)}) copy-start(s32[1024]{0:T(1024)} %param.9) | copy-start | bytes 12292
  0.6 62.2 %copy-start.1 = (u32[32]{0:T(128)S(1)}, u32[32]{0:T(128)}, u32[]{:S(2)}) copy-start(u32[32]{0:T(128)} %constant.29) | copy-start | bytes 388
  55.7 17.4 %collective-permute-start = (f32[4,2048]{1,0:T(4,128)}, f32[4,2048]{1,0:T(4,128)S(1)}, u32[]{:S(2)}, u32[]{:S(2)}) collective-permute-start(f32[4,2048]{1,0:T(4,128)} %shard_map.68), channel_id=1, source_target_pairs={{0,1},{1,2},{2,3},{3,0},{4,5},{5,6},{6,7},{7,4},{8,9},{9,10},{10,1... | collective-permute-start | bytes 98312 | tf_op jit(solution)/shard_map/ppermute | solution.py:159
  58.8 14.4 %collective-permute-start.1 = (f32[4,2048]{1,0:T(4,128)}, f32[4,2048]{1,0:T(4,128)S(1)}, u32[]{:S(2)}, u32[]{:S(2)}) collective-permute-start(f32[4,2048]{1,0:T(4,128)} %shard_map.68), channel_id=1, source_target_pairs={{0,2},{1,3},{2,0},{3,1},{4,6},{5,7},{6,4},{7,5},{8,10},{9,11},{10,... | collective-permute-start | bytes 98312 | tf_op jit(solution)/shard_map/ppermute | solution.py:159
  61.3 11.8 %collective-permute-start.2 = (f32[4,2048]{1,0:T(4,128)}, f32[4,2048]{1,0:T(4,128)S(1)}, u32[]{:S(2)}, u32[]{:S(2)}) collective-permute-start(f32[4,2048]{1,0:T(4,128)} %shard_map.68), channel_id=1, source_target_pairs={{0,3},{1,0},{2,1},{3,2},{4,7},{5,4},{6,5},{7,6},{8,11},{9,8},{10,9... | collective-permute-start | bytes 98312 | tf_op jit(solution)/shard_map/ppermute | solution.py:159

commit v14 on v13

--- a/solution.py
+++ b/solution.py
@@ -160,9 +160,14 @@
         )
     row_peak = functools.reduce(jnp.maximum, [piece[0] for piece in pieces])
     scales = [jnp.exp(piece[0] - row_peak) for piece in pieces]
-    exp_total = sum(piece[1] * s for piece, s in zip(pieces, scales))
-    moment = sum(piece[2] * s for piece, s in zip(pieces, scales))
-    chosen = sum(piece[3] for piece in pieces)
+    def same_on_every_copy(terms):
+        if len(terms) == 4:
+            return (terms[0] + terms[2]) + (terms[1] + terms[3])
+        return sum(terms)
+
+    exp_total = same_on_every_copy([piece[1] * s for piece, s in zip(pieces, scales)])
+    moment = same_on_every_copy([piece[2] * s for piece, s in zip(pieces, scales)])
+    chosen = same_on_every_copy([piece[3] for piece in pieces])
     log_total = row_peak + jnp.log(exp_total)
     expected = moment / exp_total
     logprob = jnp.where(live, chosen - log_total, 0.0)

time: 75.7 us -> 76.6 us (1.012)
  starting transfers between devices: 6.97 us -> 7.87 us
    ppermute x3, starting transfers between devices: 6.97 us -> 7.87 us  [body(): lax.ppermute(stats, 'tp', [(d, (d + shift) % group) for d in range(group)])]
where the time goes in v14:
time: 76.6 us; the launch traced here: 76.3 us
  Pallas kernels  55.1 us (72%)
  blocking collectives  8.01 us (10%)
  starting transfers between devices  7.87 us (10%)
  other arithmetic  3.13 us (4%)
  between operations  1.33 us (2%)
  local copies, waits for them, and re-layouts  0.92 us (1%)
    pallas_call x1, Pallas kernels, shard_stats(): pl.pallas_call(functools.partial(stats_kernel, row_block), grid=(vocab //...  55.1 us
    unnamed x1, blocking collectives  8.01 us
    ppermute x3, starting transfers between devices, body(): lax.ppermute(stats, 'tp', [(d, (d + shift) % group) for d in range(group)])  7.87 us
  transfers between devices with their start and end apart: 3, of which 0 were waited for; matrix products, arithmetic and copies ran while one was open for 2% of the time, Pallas kernels for 0%

profile of v14, /device:TPU:0, one launch (start us, length us, event | category | flops | bytes accessed | tf_op | source)
XLA Modules:
  0.0 76.3 jit_solution(12440748166047696576)
XLA Ops:
  0.6 0.0 copy-start
  0.6 0.0 copy-start.1
  0.7 55.1 %shard_map.68 = f32[4,2048]{1,0:T(4,128)} custom-call(f32[2048,1024]{1,0:T(8,128)} %states_ref.1, f32[1,1024]{1,0:T(1,128)} %bitcast.30, bf16[8192,1024]{1,0:T(8,128)(2,1)} %emb_ref.1, s32[1,2048]{1,0:T(1,128)} %bitcast.29), custom_call_target="tpu_custom_call" | custom-call | flops 34359738368 | bytes 25206784 | tf_op jit(solution)/shard_map/pallas_call | solution.py:121
  55.7 4.0 %collective-permute-start = (f32[4,2048]{1,0:T(4,128)}, f32[4,2048]{1,0:T(4,128)S(1)}, u32[]{:S(2)}, u32[]{:S(2)}) collective-permute-start(f32[4,2048]{1,0:T(4,128)} %shard_map.68), channel_id=1, source_target_pairs={{0,2},{1,3},{2,0},{3,1},{4,6},{5,7},{6,4},{7,5},{8,10},{9,11},{10,... | collective-permute-start | bytes 98312 | tf_op jit(solution)/shard_map/ppermute | solution.py:159
  59.8 1.6 %collective-permute-start.1 = (f32[4,2048]{1,0:T(4,128)}, f32[4,2048]{1,0:T(4,128)S(1)}, u32[]{:S(2)}, u32[]{:S(2)}) collective-permute-start(f32[4,2048]{1,0:T(4,128)} %shard_map.68), channel_id=1, source_target_pairs={{0,1},{1,2},{2,3},{3,0},{4,5},{5,6},{6,7},{7,4},{8,9},{9,10},{10,1... | collective-permute-start | bytes 98312 | tf_op jit(solution)/shard_map/ppermute | solution.py:159
  61.3 2.2 %collective-permute-start.2 = (f32[4,2048]{1,0:T(4,128)}, f32[4,2048]{1,0:T(4,128)S(1)}, u32[]{:S(2)}, u32[]{:S(2)}) collective-permute-start(f32[4,2048]{1,0:T(4,128)} %shard_map.68), channel_id=1, source_target_pairs={{0,3},{1,0},{2,1},{3,2},{4,7},{5,4},{6,5},{7,6},{8,11},{9,8},{10,9... | collective-permute-start | bytes 98312 | tf_op jit(solution)/shard_map/ppermute | solution.py:159
  63.6 0.0 copy-done
  63.6 0.1 convert_reduce_fusion
  63.7 0.0 copy-done.1
  63.7 0.6 dynamic-slice
  65.0 0.2 dynamic-update-slice
  65.2 0.1 reshape.8
  65.3 8.0 %all-reduce.1 = s32[8,8]{1,0:T(8,128)S(1)} all-reduce(s32[8,8]{1,0:T(8,128)S(1)} %reshape.8), channel_id=2, replica_groups=mesh['req'=8,'tp'=4] {'req'}, use_global_device_ids=true, to_apply=%add | all-reduce | flops 64 | bytes 512
  73.3 0.7 dynamic-slice_reduce_fusion
  74.0 0.0 collective-permute-done
  74.0 0.0 collective-permute-done.1
  74.1 0.0 collective-permute-done.2
  74.1 1.0 %fusion.3 = (f32[1,2048]{1,0:T(1,128)S(1)}, f32[1,2048]{1,0:T(1,128)S(1)}, f32[1,2048]{1,0:T(1,128)S(1)}, f32[1,2048]{1,0:T(1,128)S(1)}, f32[1,2048]{1,0:T(1,128...) fusion(f32[4,2048]{1,0:T(4,128)} %shard_map.68, ...), kind=kLoop, calls=%fused_computation.23 | loop fusion | flops 6144 | bytes 237568 | tf_op jit(solution)/shard_map/slice | solution.py:169
  75.1 1.3 %subtract_select_fusion = (f32[2048]{0:T(1024)}, f32[2048]{0:T(1024)}) fusion(f32[2048]{0:T(1024)S(1)} %bitcast.22, f32[2048]{0:T(1024)S(1)} %bitcast.21, f32[2048]{0:T(1024)S(1)} %bitcast.20, f32[2048]{0:T(1024)S(1)} %bitcast.16, s32[]{:T(128)} %dynamic-slice_reduce_fusion, f32[2048]{0:T(1024)S(1)} %bitcast.18, f32[2048]{0:T(1024)S(1)} %bitcast.28, ...), kind=kLoop, calls=%fused_computation.5 | loop fusion | flops 57344 | bytes 122884 | tf_op jit(solution)/shard_map/jit(_where)/select_n | solution.py:174
  (2 shorter events, 0.0 us)
Async XLA Ops:
  0.6 63.0 %copy-start = (s32[1024]{0:T(1024)S(1)}, s32[1024]{0:T(1024)}, u32[]{:S(2)}) copy-start(s32[1024]{0:T(1024)} %param.9) | copy-start | bytes 12292
  0.6 63.1 %copy-start.1 = (u32[32]{0:T(128)S(1)}, u32[32]{0:T(128)}, u32[]{:S(2)}) copy-start(u32[32]{0:T(128)} %constant.29) | copy-start | bytes 388
  55.7 18.3 %collective-permute-start = (f32[4,2048]{1,0:T(4,128)}, f32[4,2048]{1,0:T(4,128)S(1)}, u32[]{:S(2)}, u32[]{:S(2)}) collective-permute-start(f32[4,2048]{1,0:T(4,128)} %shard_map.68), channel_id=1, source_target_pairs={{0,2},{1,3},{2,0},{3,1},{4,6},{5,7},{6,4},{7,5},{8,10},{9,11},{10,... | collective-permute-start | bytes 98312 | tf_op jit(solution)/shard_map/ppermute | solution.py:159
  59.8 14.3 %collective-permute-start.1 = (f32[4,2048]{1,0:T(4,128)}, f32[4,2048]{1,0:T(4,128)S(1)}, u32[]{:S(2)}, u32[]{:S(2)}) collective-permute-start(f32[4,2048]{1,0:T(4,128)} %shard_map.68), channel_id=1, source_target_pairs={{0,1},{1,2},{2,3},{3,0},{4,5},{5,6},{6,7},{7,4},{8,9},{9,10},{10,1... | collective-permute-start | bytes 98312 | tf_op jit(solution)/shard_map/ppermute | solution.py:159
  61.3 12.7 %collective-permute-start.2 = (f32[4,2048]{1,0:T(4,128)}, f32[4,2048]{1,0:T(4,128)S(1)}, u32[]{:S(2)}, u32[]{:S(2)}) collective-permute-start(f32[4,2048]{1,0:T(4,128)} %shard_map.68), channel_id=1, source_target_pairs={{0,3},{1,0},{2,1},{3,2},{4,7},{5,4},{6,5},{7,6},{8,11},{9,8},{10,9... | collective-permute-start | bytes 98312 | tf_op jit(solution)/shard_map/ppermute | solution.py:159
